TPU v7x, 256 devices: a whole 4x4x8 slice. The times are simulated.
256 devices in a mesh: req: 64 (over y, z_lo, x, core), tp: 4 (over z_hi).
Axes of the slice: x: 4, y: 4, z: 8 (z_hi: 4, z_lo: 2; z = z_hi * 2 + z_lo), core: 2. Of those that a mesh axis runs over, the one named last changes fastest.
Arguments:
- tokens: bfloat16 [16384, 2048], P('req'), may hold values from -6 to 6
- norm_gain: float32 [2048], replicated, may hold values from 0.25 to 1.75
- w_query: bfloat16 [2048, 2048], P(None, 'tp'), may hold values from -1 to 1
- w_key: bfloat16 [2048, 2048], P(None, 'tp'), may hold values from -1 to 1
- w_value: bfloat16 [2048, 2048], P(None, 'tp'), may hold values from -0.125 to 0.125
- w_out: bfloat16 [2048, 2048], P('tp'), may hold values from -0.125 to 0.125
- lambdas: float32 [4, 8, 128], P(None, 'tp'), may hold values from -1 to 1
- sub_gain: float32 [8, 256], P('tp'), may hold values from 0.5 to 2
- lengths: int32 [4], replicated, may hold values from 1 to 8192, 16384 in all
Outputs:
- hidden: bfloat16 [16384, 2048], P('req')
- key_cache: bfloat16 [16384, 2048], P('req', 'tp')
- value_cache: bfloat16 [16384, 2048], P('req', 'tp')
Inputs may be any that keep to these rules, and one draw needn't show every extreme that they name: The lengths sum to 16384; the longest is exactly 8192.
All inputs are finite; a program needn't handle non-finite values.
Results may differ from a plain program's by a relative error of at most 0.007.
Values may be sent and summed in bfloat16 or wider, within the bound.
No kernel may reach another device: no remote copies, remote signals or barrier semaphores. Data moves between devices by JAX's collectives and lax.ppermute only.
A program may use at most 128 MiB of HBM per device.

v0:
```python
import math

import jax
import jax.numpy as jnp
from jax import lax
from jax.sharding import Mesh
from jax.sharding import PartitionSpec as P

QK = 128
VD = 256
MAXLEN = 8192


lambda_start = 0.8 - 0.6 * math.exp(-3.3)
masked_score = -1e30


def locate(index, lengths):
    ends = jnp.cumsum(lengths)
    starts = ends - lengths
    segment = jnp.sum((ends[None, :] <= index[:, None]).astype(jnp.int32), axis=1)
    hit = jnp.arange(lengths.shape[0], dtype=jnp.int32)[None, :] == segment[:, None]
    begin = jnp.sum(jnp.where(hit, starts[None, :], 0), axis=1)
    return (segment, index - begin)


def rotate(proj, position):
    half = proj.shape[-1] // 2
    freq = 10000.0 ** (-jnp.arange(half, dtype=jnp.float32) / half)
    angle = position.astype(jnp.float32)[:, None] * freq[None, :]
    cosine = jnp.cos(angle)[:, None, None, :]
    sine = jnp.sin(angle)[:, None, None, :]
    front = proj[..., :half]
    back = proj[..., half:]
    return jnp.concatenate([front * cosine - back * sine, back * cosine + front * sine], axis=-1)


def swap_cores(value):
    return lax.ppermute(value, "core", [(0, 1), (1, 0)])


def on_device(tokens, norm_gain, w_query, w_key, w_value, w_out, lambdas, sub_gain, lengths):
    rows = tokens.shape[0]
    heads = w_query.shape[1] // (2 * QK)
    key_cols = heads * 2 * QK
    ys, zs, xs = lax.axis_size("y"), lax.axis_size("z"), lax.axis_size("x")
    chips = ys * zs * xs
    total = rows * 2 * chips
    core = lax.axis_index("core")
    chip = (lax.axis_index("y") * zs + lax.axis_index("z")) * xs + lax.axis_index("x")
    first = (chip * 2 + core) * rows
    local_index = first + jnp.arange(rows, dtype=jnp.int32)
    unused, pos_own = locate(local_index, lengths)
    xf = tokens.astype(jnp.float32)
    normed = (xf * lax.rsqrt(jnp.mean(xf * xf, axis=-1, keepdims=True) + 1e-06) * norm_gain).astype(
        jnp.bfloat16
    )
    keys = rotate(
        jnp.dot(normed, w_key, preferred_element_type=jnp.float32).reshape(rows, heads, 2, QK),
        pos_own,
    ).astype(jnp.bfloat16)
    values = jnp.dot(normed, w_value, preferred_element_type=jnp.float32).astype(jnp.bfloat16)
    key_flat = keys.reshape(rows, key_cols)
    lam = (
        jnp.exp(jnp.sum(lambdas[0] * lambdas[1], axis=-1))
        - jnp.exp(jnp.sum(lambdas[2] * lambdas[3], axis=-1))
        + lambda_start
    )
    scale = QK ** (-0.5)

    def head_kv(h):
        k_h = lax.dynamic_index_in_dim(keys, h, axis=1, keepdims=False).reshape(rows, 2 * QK)
        v_h = lax.dynamic_index_in_dim(values.reshape(rows, heads, VD), h, axis=1, keepdims=False)
        return jnp.concatenate([k_h, v_h], axis=1)

    def in_order(mine, theirs):
        return jnp.where(core == 0, jnp.concatenate([mine, theirs], axis=0), jnp.concatenate([theirs, mine], axis=0))

    span = 2 * rows
    kv_pair = in_order(head_kv(core), swap_cores(head_kv(1 - core)))
    z = lax.axis_index("z")
    kv_z = lax.ppermute(kv_pair, "z", [(0, 1), (1, 0)])
    kv_quad = jnp.where(z == 0, jnp.concatenate([kv_pair, kv_z], axis=0), jnp.concatenate([kv_z, kv_pair], axis=0))
    gathered = lax.all_gather(kv_quad, ("y", "x"), axis=0, tiled=True)
    query = rotate(
        jnp.dot(normed, w_query, preferred_element_type=jnp.float32).reshape(rows, heads, 2, QK),
        pos_own,
    ).astype(jnp.bfloat16)
    q_pair = in_order(
        lax.dynamic_index_in_dim(query, core, axis=1, keepdims=False),
        swap_cores(lax.dynamic_index_in_dim(query, 1 - core, axis=1, keepdims=False)),
    )

    reach = min(MAXLEN // span + 1, chips)
    window = reach * span
    base = chip * span
    first_chip = jnp.clip(chip + 1 - reach, 0, chips - reach)
    start = first_chip * span
    blocks = []
    for i in range(reach):
        c = first_chip + i
        slot = ((c // (zs * xs)) * xs + c % xs) * zs + (c // xs) % zs
        blocks.append(lax.dynamic_slice_in_dim(gathered, slot * span, span, axis=0))
    kv_window = jnp.concatenate(blocks, axis=0)
    q_index = base + jnp.arange(span, dtype=jnp.int32)
    q_seg, unused = locate(q_index, lengths)
    pieces = 2
    piece = window // pieces

    def part(p):
        key_index = start + p * piece + jnp.arange(piece, dtype=jnp.int32)
        k_seg, unused = locate(key_index, lengths)
        allowed = (key_index[None, :] <= q_index[:, None]) & (k_seg[None, :] == q_seg[:, None])
        kv_win = kv_window[p * piece : (p + 1) * piece]
        v_win = kv_win[:, 2 * QK :]
        stats = []
        for m in range(2):
            k_m = kv_win[:, m * QK : (m + 1) * QK]
            scores = jnp.einsum("qd,kd->qk", q_pair[:, m, :], k_m, preferred_element_type=jnp.float32) * scale
            scores = jnp.where(allowed, scores, masked_score)
            top = jnp.max(scores, axis=-1, keepdims=True)
            weights = jnp.where(allowed, jnp.exp(scores - top), 0.0)
            mass = jnp.sum(weights, axis=-1, keepdims=True)
            acc = jnp.dot(weights.astype(jnp.bfloat16), v_win, preferred_element_type=jnp.float32)
            stats.append((top, mass, acc))
        return stats

    all_stats = [part(p) for p in range(pieces)]

    def attend(m):
        tops = [stats[m][0] for stats in all_stats]
        top = tops[0]
        for other in tops[1:]:
            top = jnp.maximum(top, other)
        acc = 0.0
        mass = 0.0
        for stats in all_stats:
            fade = jnp.exp(stats[m][0] - top)
            mass = mass + stats[m][1] * fade
            acc = acc + stats[m][2] * fade
        return acc / mass

    lam_h = lax.dynamic_index_in_dim(lam, core, keepdims=False)
    gain_h = lax.dynamic_index_in_dim(sub_gain, core, axis=0, keepdims=False)
    diff = attend(0) - lam_h * attend(1)
    head_out = (
        diff * lax.rsqrt(jnp.mean(diff * diff, axis=-1, keepdims=True) + 1e-05) * gain_h * (1.0 - lambda_start)
    ).astype(jnp.bfloat16)
    own_rows = lax.dynamic_slice_in_dim(head_out, core * rows, rows, axis=0)
    other_rows = swap_cores(lax.dynamic_slice_in_dim(head_out, (1 - core) * rows, rows, axis=0))
    merged = jnp.where(
        core == 0,
        jnp.concatenate([own_rows, other_rows], axis=1),
        jnp.concatenate([other_rows, own_rows], axis=1),
    )
    summed = lax.psum(
        jnp.dot(merged, w_out, preferred_element_type=jnp.float32).astype(jnp.bfloat16), "tp"
    ).astype(jnp.float32)
    hidden = (xf + summed).astype(jnp.bfloat16)
    return (hidden, key_flat, values)


def solution(mesh):
    req, tp = mesh.shape["req"], mesh.shape["tp"]
    paired = Mesh(mesh.devices.reshape(req // 16, 2, 4, 2, tp), ("y", "z", "x", "core", "tp"))
    rows = ("y", "z", "x", "core")
    in_specs = (
        P(rows, None),
        P(),
        P(None, "tp"),
        P(None, "tp"),
        P(None, "tp"),
        P("tp", None),
        P(None, "tp", None),
        P("tp", None),
        P(),
    )
    out_specs = (P(rows, None), P(rows, "tp"), P(rows, "tp"))
    return jax.shard_map(
        on_device, mesh=paired, in_specs=in_specs, out_specs=out_specs, check_vma=False
    )
```

profile of v0, /device:TPU:1, one launch (start us, length us, event | category | flops | bytes accessed | tf_op | source)
XLA Modules:
  0.0 312.1 jit_solution(18068048062098349689)
XLA Ops:
  9.1 1.5 fusion.24
  10.6 2.7 fusion.104
  17.2 3.4 %convolution_convert_fusion.1 = bf16[256,512]{1,0:T(8,128)(2,1)} fusion(bf16[2048,512]{1,0:T(8,128)(2,1)} %param.13, bf16[256,2048]{1,0:T(8,128)(2,1)} %param.9, f32[2048]{0:T(1024)S(1)} %copy-done.12, f32[256]{0:T(256)S(1)} %add_rsqrt_fusion.1), kind=kOutput, calls=%fused_computation.48 | convolution fusion | flops 539099136 | bytes 3417088 | tf_op jit(solution)/shard_map/dot_general | solution.py:62
  20.6 1.1 reshape.230
  21.7 1.3 constant_dynamic-slice_fusion.5
  23.0 1.6 pad_maximum_fusion
  24.6 3.2 %collective-permute-start.1 = (bf16[256,512]{1,0:T(8,128)(2,1)}, bf16[256,512]{1,0:T(8,128)(2,1)}, u32[]{:S(2)}, u32[]{:S(2)}) collective-permute-start(bf16[256,512]{1,0:T(8,128)(2,1)} %pad_maximum_fusion), channel_id=1, source_target_pairs={{0,4},{4,0},{1,5},{5,1},{2,6},{6,2},{3,7},{7,3},{8,12},{12,8},{9,1... | collective-permute-start | bytes 786440 | tf_op jit(solution)/shard_map/ppermute | solution.py:39
  29.8 2.0 maximum_select_fusion.1
  31.8 13.9 %collective-permute-done.2 = bf16[512,512]{1,0:T(8,128)(2,1)} collective-permute-done((bf16[512,512]{1,0:T(8,128)(2,1)}, bf16[512,512]{1,0:T(8,128)(2,1)}, u32[]{:S(2)}, u32[]{:S(2)}) %collective-permute-start.2) | collective-permute-done | bytes 524320 | tf_op jit(solution)/shard_map/ppermute | solution.py:82
  45.6 2.8 maximum_select_fusion
  48.5 3.1 %fusion.106 = f32[256,512]{1,0:T(8,128)} fusion(bf16[2048,512]{1,0:T(8,128)(2,1)} %param.11, bf16[256,2048]{1,0:T(8,128)(2,1)S(1)} %copy-done.1, f32[2048]{0:T(1024)S(1)} %copy-done.12, f32[256]{0:T(256)S(1)} %add_rsqrt_fusion.1), kind=kOutput, calls=%fused_computation.150 | convolution fusion | flops 538968064 | bytes 3679232 | tf_op jit(solution)/shard_map/dot_general | solution.py:86
  51.6 1.4 reshape.227
  56.8 109.4 %all-gather.2.cloned.1.call-done = bf16[16384,512]{1,0:T(8,128)(2,1)} async-done(((bf16[1024,512]{1,0:T(8,128)(2,1)}), bf16[16384,512]{1,0:T(8,128)(2,1)}) %all-gather.2.cloned.1.call-update) | async-done | bytes 16777232 | tf_op jit(solution)/shard_map/all_gather | solution.py:84
  167.3 1.1 dynamic-slice_dynamic-update-slice_fusion.14
  168.4 1.1 dynamic-slice_dynamic-update-slice_fusion.13
  170.6 1.1 dynamic-slice_dynamic-update-slice_fusion.11
  171.7 1.1 dynamic-slice_dynamic-update-slice_fusion.10
  174.9 1.1 dynamic-slice_dynamic-update-slice_fusion.17
  176.1 1.5 dynamic-slice_dynamic-update-slice_fusion.7
  177.6 1.4 dynamic-slice_dynamic-update-slice_fusion.6
  185.5 5.1 %fusion.115 = (f32[512]{0:T(512)S(1)}, f32[512,4352]{1,0:T(8,128)}) fusion(bf16[4608,512]{1,0:T(8,128)(2,1)S(1)} %dynamic-slice_dynamic-update-slice_fusion, bf16[512,2,128]{2,0,1:T(8,128)(2,1)S(1)} %maximum_select_fusion.2, s32[512]{0:T(512)S(1)} %convert_reduce_fusion.2, s32[4352]{0:T(1024)S(1)} %get-tuple-element.12, s32[512]{0:T(512)S(1)} %iota_add_fusion.2, ...), kind=kOutput, calls=%fused_computation.154 | convolution fusion | flops 583794176 | bytes 10205184 | tf_op jit(solution)/shard_map/qd,kd->qk/dot_general | solution.py:119
  190.5 2.6 fusion.112
  193.2 2.6 fusion.113
  195.8 3.5 %fusion.114 = (f32[512]{0:T(512)S(1)}, f32[512,4352]{1,0:T(8,128)S(1)}) fusion(bf16[4608,512]{1,0:T(8,128)(2,1)S(1)} %get-tuple-element.19, bf16[512,2,128]{2,0,1:T(8,128)(2,1)} %copy-done.7, s32[512]{0:T(512)S(1)} %convert_reduce_fusion.2, s32[4352]{0:T(1024)S(1)} %get-tuple-element.11, s32[512]{0:T(512)S(1)} %iota_add_fusion.2, ...), kind=kOutput, calls=%fused_computation.153 | convolution fusion | flops 583794176 | bytes 10205184 | tf_op jit(solution)/shard_map/qd,kd->qk/dot_general | solution.py:119
  199.3 11.1 %fusion.4 = (f32[512]{0:T(512)S(1)}, f32[512]{0:T(512)S(1)}, f32[512]{0:T(512)S(1)}, f32[512]{0:T(512)S(1)}) fusion(f32[512,4352]{1,0:T(8,128)S(1)} %get-tuple-element.38, f32[512]{0:T(512)S(1)} %get-tuple-element.37, s32[512]{0:T(512)S(1)} %convert_reduce_fusion.2, s32[4352]{0:T(1024)S(1)} %get-tuple-element.11, s32[512]{0:T(512)S(1)} %iota_add_fusion.2, ...), kind=kLoop, calls=%fused_computation.14 | loop fusion | flops 40105984 | bytes 35741696 | tf_op jit(solution)/shard_map/reduce_sum | solution.py:123
  210.4 7.5 %fusion.57 = f32[512,256]{0,1:T(8,128)} fusion(bf16[4608,512]{1,0:T(8,128)(2,1)} %copy-done.8, f32[512,4352]{1,0:T(8,128)} %get-tuple-element.42, f32[512]{0:T(512)S(1)} %get-tuple-element.41, f32[512]{0:T(512)S(1)} %get-tuple-element.15, s32[4352]{0:T(1024)S(1)} %get-tuple-element.12, s32[4352]{0:T(1024)S(1)} %get-tuple-element.45, ...), kind=kOutput, calls=%fused_computation.47 | convolution fusion | flops 1154351104 | bytes 11708416 | tf_op jit(solution)/shard_map/dot_general | solution.py:124
  217.9 4.4 %fusion.42 = f32[512,256]{0,1:T(8,128)S(1)} fusion(bf16[4608,512]{1,0:T(8,128)(2,1)} %copy-done.8, f32[512,4352]{1,0:T(8,128)S(1)} %get-tuple-element.36, f32[512]{0:T(512)S(1)} %get-tuple-element.35, f32[512]{0:T(512)S(1)} %get-tuple-element.18, s32[4352]{0:T(1024)S(1)} %get-tuple-element.12, s32[4352]{0:T(1024)S(1)} %get-tuple-element.45, ...), kind=kOutput, calls=%fused_computation.44 | convolution fusion | flops 1154351104 | bytes 11708416 | tf_op jit(solution)/shard_map/dot_general | solution.py:124
  222.4 4.5 %fusion.81 = f32[512,256]{0,1:T(8,128)S(1)} fusion(f32[512,256]{0,1:T(8,128)S(1)} %fusion.42, bf16[4608,512]{1,0:T(8,128)(2,1)} %copy-done.9, f32[512,4352]{1,0:T(8,128)S(1)} %get-tuple-element.40, f32[512]{0:T(512)S(1)} %get-tuple-element.39, f32[512]{0:T(512)S(1)} %get-tuple-element.16, f32[512]{0:T(512)S(1)} %get-tuple-element.17, ...), kind=kOutput, calls=%fused_computation.57 | convolution fusion | flops 1154613248 | bytes 12234752 | tf_op jit(solution)/shard_map/dot_general | solution.py:124
  226.8 5.1 %multiply_reduce_fusion = (f32[512]{0:T(512)S(1)}, f32[512,256]{0,1:T(8,128)S(1)}) fusion(f32[512,256]{0,1:T(8,128)S(1)} %fusion.81, f32[512]{0:T(512)S(1)} %get-tuple-element.13, f32[512,256]{0,1:T(8,128)S(1)} %copy-done.13, f32[512]{0:T(512)S(1)} %get-tuple-element.14, bf16[4608,512]{1,0:T(8,128)(2,1)} %copy-done.9, ...), kind=kOutput, calls=%fused_computation.61 | convolution fusion | flops 1155137024 | bytes 12761600 | tf_op jit(solution)/shard_map/dot_general | solution.py:124
  234.0 1.7 convolution_convert_fusion
  236.5 66.2 %all-reduce.2.cloned.1.call-done = bf16[256,2048]{1,0:T(8,128)(2,1)} async-done(((bf16[256,2048]{1,0:T(8,128)(2,1)}), bf16[256,2048]{1,0:T(8,128)(2,1)}) %all-reduce.2.cloned.1.call-update) | async-done | bytes 1048592 | tf_op jit(solution)/shard_map/psum | solution.py:156
  302.7 2.6 fusion.27
  (84 shorter events, 25.0 us)
Async XLA Ops:
  7.2 226.8 %copy-start = (bf16[512,2048]{1,0:T(8,128)(2,1)S(1)}, bf16[512,2048]{1,0:T(8,128)(2,1)}, u32[]{:S(2)}) copy-start(bf16[512,2048]{1,0:T(8,128)(2,1)} %param.14) | copy-start | bytes 6291460
  7.2 159.1 %all-gather.2.cloned.1.call-start = ((), (), s32[]{:S(2)}) async-start(), calls=%async_computation | async-start | bytes 17825792 | tf_op jit(solution)/shard_map/all_gather | solution.py:84
  10.6 6.6 %copy-start.12 = (f32[2048]{0:T(1024)S(1)}, f32[2048]{0:T(1024)}, u32[]{:S(2)}) copy-start(f32[2048]{0:T(1024)} %param.10) | copy-start | bytes 24580
  14.2 3.0 copy-start.5
  15.7 1.5 copy-start.3
  20.6 27.9 %copy-start.1 = (bf16[256,2048]{1,0:T(8,128)(2,1)S(1)}, bf16[256,2048]{1,0:T(8,128)(2,1)}, u32[]{:S(2)}) copy-start(bf16[256,2048]{1,0:T(8,128)(2,1)} %param.9) | copy-start | bytes 3145732
  24.6 5.1 %collective-permute-start.1 = (bf16[256,512]{1,0:T(8,128)(2,1)}, bf16[256,512]{1,0:T(8,128)(2,1)}, u32[]{:S(2)}, u32[]{:S(2)}) collective-permute-start(bf16[256,512]{1,0:T(8,128)(2,1)} %pad_maximum_fusion), channel_id=1, source_target_pairs={{0,4},{4,0},{1,5},{5,1},{2,6},{6,2},{3,7},{7,3},{8,12},{12,8},{9,1... | collective-permute-start | bytes 786440 | tf_op jit(solution)/shard_map/ppermute | solution.py:39
  29.7 23.3 %copy-start.6 = (f32[256,64]{1,0:T(8,128)S(1)}, f32[256,64]{1,0:T(8,128)}, u32[]{:S(2)}) copy-start(f32[256,64]{1,0:T(8,128)} %copy-done.5) | copy-start | bytes 196612
  31.7 13.9 %collective-permute-start.2 = (bf16[512,512]{1,0:T(8,128)(2,1)}, bf16[512,512]{1,0:T(8,128)(2,1)}, u32[]{:S(2)}, u32[]{:S(2)}) collective-permute-start(bf16[512,512]{1,0:T(8,128)(2,1)} %maximum_select_fusion.1), channel_id=1, source_target_pairs={{0,32},{32,0},{1,33},{33,1},{2,34},{34,2},{3,35},{35,3},{4,36},{36... | collective-permute-start | bytes 1572872 | tf_op jit(solution)/shard_map/ppermute | solution.py:82
  48.4 7.0 %copy-start.11 = (f32[2,256]{1,0:T(2,128)S(1)}, f32[2,256]{1,0:T(2,128)}, u32[]{:S(2)}) copy-start(f32[2,256]{1,0:T(2,128)} %param.16) | copy-start | bytes 6148
  48.4 7.0 %copy-start.10 = (f32[4,2,128]{2,1,0:T(2,128)S(1)}, f32[4,2,128]{2,1,0:T(2,128)}, u32[]{:S(2)}) copy-start(f32[4,2,128]{2,1,0:T(2,128)} %param.15) | copy-start | bytes 12292
  48.4 254.3 %all-reduce.2.cloned.1.call-start = ((), (), s32[]{:S(2)}) async-start(), calls=%async_computation.1 | async-start | bytes 2097152 | tf_op jit(solution)/shard_map/psum | solution.py:156
  54.6 2.2 collective-permute-start
  56.8 136.3 %copy-start.7 = (bf16[512,2,128]{2,0,1:T(8,128)(2,1)}, bf16[512,2,128]{2,0,1:T(8,128)(2,1)S(1)}, u32[]{:S(2)}) copy-start(bf16[512,2,128]{2,0,1:T(8,128)(2,1)S(1)} %maximum_select_fusion.2) | copy-start | bytes 786436
  176.1 19.8 %copy-start.9 = (bf16[4608,512]{1,0:T(8,128)(2,1)}, bf16[4608,512]{1,0:T(8,128)(2,1)S(1)}, u32[]{:S(2)}) copy-start(bf16[4608,512]{1,0:T(8,128)(2,1)S(1)} %get-tuple-element.19) | copy-start | bytes 14155780
  185.4 5.1 %copy-start.8 = (bf16[4608,512]{1,0:T(8,128)(2,1)}, bf16[4608,512]{1,0:T(8,128)(2,1)S(1)}, u32[]{:S(2)}) copy-start(bf16[4608,512]{1,0:T(8,128)(2,1)S(1)} %dynamic-slice_dynamic-update-slice_fusion) | copy-start | bytes 14155780
  222.4 4.5 %copy-start.13 = (f32[512,256]{0,1:T(8,128)S(1)}, f32[512,256]{0,1:T(8,128)}, u32[]{:S(2)}) copy-start(f32[512,256]{0,1:T(8,128)} %fusion.57) | copy-start | bytes 1572868
  231.9 3.8 %copy-start.4 = (bf16[256,2,2,128]{3,2,1,0:T(2,128)(2,1)S(1)}, bf16[256,2,2,128]{3,2,1,0:T(2,128)(2,1)}, u32[]{:S(2)}) copy-start(bf16[256,2,2,128]{3,2,1,0:T(2,128)(2,1)} %copy-done.3) | copy-start | bytes 786436
  232.0 70.8 %copy-start.2 = (bf16[256,2048]{1,0:T(8,128)(2,1)S(1)}, bf16[256,2048]{1,0:T(8,128)(2,1)}, u32[]{:S(2)}) copy-start(bf16[256,2048]{1,0:T(8,128)(2,1)} %param.9) | copy-start | bytes 3145732
  232.1 1.8 collective-permute-start.3
Sparse Core Ops, SparseCore 0:
  48.5 117.6 all-gather.1
  235.8 66.8 all-reduce.1
where the time goes:
time: 313 us; the launch traced here: 312 us
  waiting for transfers between devices  190 us (61%)
  matrix products  46.2 us (15%)
  local copies, waits for them, and re-layouts  28.2 us (9%)
  other arithmetic  27.5 us (9%)
  between operations  14.7 us (5%)
  starting transfers between devices  5.04 us (2%)
    all_gather x1, waiting for transfers between devices, on_device(): gathered = lax.all_gather(kv_quad, ('y', 'x'), axis=0, tiled=True)  109 us
    psum x1, waiting for transfers between devices, on_device(): lax.psum(jnp.dot(merged, w_out, preferred_element_type=jnp.float32).astyp...  66.2 us
    dot_general x4, matrix products, part(): jnp.dot(weights.astype(jnp.bfloat16), v_win, preferred_element_type=jnp.f...  21.5 us
    unnamed x47, local copies, waits for them, and re-layouts  19.6 us
    ppermute x1, waiting for transfers between devices, on_device(): kv_z = lax.ppermute(kv_pair, 'z', [(0, 1), (1, 0)])  13.9 us
    dot_general x4, matrix products, part(): jnp.einsum('qd,kd->qk', q_pair[:, m, :], k_m, preferred_element_type=jnp....  13.8 us
    reduce_sum x1, other arithmetic, part(): mass = jnp.sum(weights, axis=-1, keepdims=True)  11.1 us
  transfers between devices with their start and end apart: 6, of which 4 were waited for; matrix products, arithmetic and copies ran while one was open for 3% of the time, Pallas kernels for 0%

commit v1 on v0

--- a/solution.py
+++ b/solution.py
@@ -96,12 +96,9 @@
     base = chip * span
     first_chip = jnp.clip(chip + 1 - reach, 0, chips - reach)
     start = first_chip * span
-    blocks = []
-    for i in range(reach):
-        c = first_chip + i
-        slot = ((c // (zs * xs)) * xs + c % xs) * zs + (c // xs) % zs
-        blocks.append(lax.dynamic_slice_in_dim(gathered, slot * span, span, axis=0))
-    kv_window = jnp.concatenate(blocks, axis=0)
+    c = first_chip + jnp.arange(reach, dtype=jnp.int32)
+    slot = ((c // (zs * xs)) * xs + c % xs) * zs + (c // xs) % zs
+    kv_window = jnp.take(gathered.reshape(chips, span, -1), slot, axis=0, mode="clip").reshape(window, -1)
     q_index = base + jnp.arange(span, dtype=jnp.int32)
     q_seg, unused = locate(q_index, lengths)
     pieces = 2

time: 313 us -> 310 us (level)
  local copies, waits for them, and re-layouts: 28.2 us -> 22.1 us
  matrix products: 46.2 us -> 49.6 us
    unnamed x47 -> x26, local copies, waits for them, and re-layouts: 19.6 us -> 3.27 us
    gather x0 -> x1, local copies, waits for them, and re-layouts: none -> 10.7 us  [on_device(): jnp.take(gathered.reshape(chips, span, -1), slot, axis=0, mode='clip')]
    dot_general x4, matrix products: 13.8 us -> 17.2 us  [part(): jnp.einsum('qd,kd->qk', q_pair[:, m, :], k_m, preferred_element_type=jnp....]
where the time goes in v1:
time: 310 us
  waiting for transfers between devices  189 us (61%)
  matrix products  49.6 us (16%)
  other arithmetic  29.1 us (9%)
  local copies, waits for them, and re-layouts  22.1 us (7%)
  between operations  14.4 us (5%)
  starting transfers between devices  5.18 us (2%)
    all_gather x1, waiting for transfers between devices, on_device(): gathered = lax.all_gather(kv_quad, ('y', 'x'), axis=0, tiled=True)  108 us
    psum x1, waiting for transfers between devices, on_device(): lax.psum(jnp.dot(merged, w_out, preferred_element_type=jnp.float32).astyp...  66.1 us
    dot_general x4, matrix products, part(): jnp.dot(weights.astype(jnp.bfloat16), v_win, preferred_element_type=jnp.f...  21.4 us
    dot_general x4, matrix products, part(): jnp.einsum('qd,kd->qk', q_pair[:, m, :], k_m, preferred_element_type=jnp....  17.2 us
    ppermute x1, waiting for transfers between devices, on_device(): kv_z = lax.ppermute(kv_pair, 'z', [(0, 1), (1, 0)])  13.9 us
    reduce_sum x1, other arithmetic, part(): mass = jnp.sum(weights, axis=-1, keepdims=True)  11.7 us
    gather x1, local copies, waits for them, and re-layouts, on_device(): jnp.take(gathered.reshape(chips, span, -1), slot, axis=0, mode='clip')  10.7 us
  transfers between devices with their start and end apart: 6, of which 4 were waited for; matrix products, arithmetic and copies ran while one was open for 3% of the time, Pallas kernels for 0%

profile of v1, /device:TPU:1, one launch (start us, length us, event | category | flops | bytes accessed | tf_op | source)
XLA Modules:
  0.0 309.8 jit_solution(10893545579468635944)
XLA Ops:
  7.3 1.0 reduce-window.8
  9.1 1.5 fusion.24
  10.6 2.7 fusion.110
  17.8 3.4 %convolution_convert_fusion.1 = bf16[256,512]{1,0:T(8,128)(2,1)} fusion(bf16[2048,512]{1,0:T(8,128)(2,1)} %param.13, bf16[256,2048]{1,0:T(8,128)(2,1)} %param.9, f32[2048]{0:T(1024)} %param.10, f32[256]{0:T(256)S(1)} %add_rsqrt_fusion.1), kind=kOutput, calls=%fused_computation.49 | convolution fusion | flops 539099136 | bytes 3417088 | tf_op jit(solution)/shard_map/dot_general | solution.py:62
  21.2 1.7 reshape.382
  23.0 2.3 constant_dynamic-slice_fusion.5
  25.3 1.6 pad_maximum_fusion
  26.9 3.2 %collective-permute-start.1 = (bf16[256,512]{1,0:T(8,128)(2,1)}, bf16[256,512]{1,0:T(8,128)(2,1)}, u32[]{:S(2)}, u32[]{:S(2)}) collective-permute-start(bf16[256,512]{1,0:T(8,128)(2,1)} %pad_maximum_fusion), channel_id=1, source_target_pairs={{0,4},{4,0},{1,5},{5,1},{2,6},{6,2},{3,7},{7,3},{8,12},{12,8},{9,1... | collective-permute-start | bytes 786440 | tf_op jit(solution)/shard_map/ppermute | solution.py:39
  30.2 0.9 copy.31
  31.1 1.0 copy.33
  32.1 2.0 maximum_select_fusion.1
  34.0 13.9 %collective-permute-done.2 = bf16[512,512]{1,0:T(8,128)(2,1)} collective-permute-done((bf16[512,512]{1,0:T(8,128)(2,1)}, bf16[512,512]{1,0:T(8,128)(2,1)}, u32[]{:S(2)}, u32[]{:S(2)}) %collective-permute-start.2) | collective-permute-done | bytes 524320 | tf_op jit(solution)/shard_map/ppermute | solution.py:82
  47.9 2.8 maximum_select_fusion
  50.8 3.2 %fusion.112 = f32[256,512]{1,0:T(8,128)} fusion(bf16[2048,512]{1,0:T(8,128)(2,1)} %param.11, bf16[256,2048]{1,0:T(8,128)(2,1)S(1)} %copy-done.2, f32[2048]{0:T(1024)} %param.10, f32[256]{0:T(256)S(1)} %add_rsqrt_fusion.1), kind=kOutput, calls=%fused_computation.152 | convolution fusion | flops 538968064 | bytes 3679232 | tf_op jit(solution)/shard_map/dot_general | solution.py:86
  53.9 1.4 reshape.379
  55.3 1.7 add_convert_fusion
  57.7 1.1 collective-permute-start
  60.0 108.5 %all-gather.2.cloned.1.call-done = bf16[16384,512]{1,0:T(8,128)(2,1)} async-done(((bf16[1024,512]{1,0:T(8,128)(2,1)}), bf16[16384,512]{1,0:T(8,128)(2,1)}) %all-gather.2.cloned.1.call-update) | async-done | bytes 16777232 | tf_op jit(solution)/shard_map/all_gather | solution.py:84
  168.5 10.7 %gather_fusion = bf16[17,512,512]{2,1,0:T(8,128)(2,1)} fusion(bf16[32,512,512]{2,1,0:T(8,128)(2,1)} %bitcast.59, s32[1024]{0:T(1024)S(1)} %pad_clamp_fusion), kind=kCustom, calls=%fused_computation | custom fusion | bytes 17825860 | tf_op jit(solution)/shard_map/jit(_take)/gather | solution.py:101
  179.2 4.0 %fusion.119 = (f32[512]{0:T(512)S(1)}, f32[512,4352]{1,0:T(8,128)S(1)}) fusion(bf16[8704,512]{1,0:T(8,128)(2,1)} %bitcast.51, bf16[512,2,128]{2,0,1:T(8,128)(2,1)S(1)} %maximum_select_fusion.2, s32[512]{0:T(512)S(1)} %convert_reduce_fusion.2, s32[4352]{0:T(1024)S(1)} %get-tuple-element.11, s32[512]{0:T(512)S(1)} %iota_add_fusion.2, ...), kind=kOutput, calls=%fused_computation.154 | convolution fusion | flops 583794176 | bytes 10205184 | tf_op jit(solution)/shard_map/qd,kd->qk/dot_general | solution.py:116
  183.2 3.6 %fusion.120 = (f32[512]{0:T(512)S(1)}, f32[512,4352]{1,0:T(8,128)S(1)}) fusion(bf16[8704,512]{1,0:T(8,128)(2,1)S(1)} %bitcast.52, bf16[512,2,128]{2,0,1:T(8,128)(2,1)} %copy-done.7, s32[512]{0:T(512)S(1)} %convert_reduce_fusion.2, s32[4352]{0:T(1024)S(1)} %get-tuple-element.11, s32[512]{0:T(512)S(1)} %iota_add_fusion.2, s32[4352]{0:T(1024)S(1)} %get-tuple-element.44), kind=kOutput, calls=%fused_computation.155 | convolution fusion | flops 583794176 | bytes 10205184 | tf_op jit(solution)/shard_map/qd,kd->qk/dot_general | solution.py:116
  186.8 4.9 %fusion.121 = (f32[512]{0:T(512)S(1)}, f32[512,4352]{1,0:T(8,128)}) fusion(bf16[8704,512]{1,0:T(8,128)(2,1)S(1)} %bitcast.53, bf16[512,2,128]{2,0,1:T(8,128)(2,1)S(1)} %copy-done.8, s32[512]{0:T(512)S(1)} %convert_reduce_fusion.2, s32[4352]{0:T(1024)S(1)} %get-tuple-element.12, s32[512]{0:T(512)S(1)} %iota_add_fusion.2, s32[4352]{0:T(1024)S(1)} %get-tuple-element.43), kind=kOutput, calls=%fused_computation.156 | convolution fusion | flops 583794176 | bytes 10205184 | tf_op jit(solution)/shard_map/qd,kd->qk/dot_general | solution.py:116
  191.6 4.9 %fusion.118 = (f32[512]{0:T(512)S(1)}, f32[512,4352]{1,0:T(8,128)}) fusion(bf16[8704,512]{1,0:T(8,128)(2,1)S(1)} %bitcast.54, bf16[512,2,128]{2,0,1:T(8,128)(2,1)S(1)} %copy-done.8, s32[512]{0:T(512)S(1)} %convert_reduce_fusion.2, s32[4352]{0:T(1024)S(1)} %get-tuple-element.12, s32[512]{0:T(512)S(1)} %iota_add_fusion.2, s32[4352]{0:T(1024)S(1)} %get-tuple-element.43), kind=kOutput, calls=%fused_computation.153 | convolution fusion | flops 583794176 | bytes 10205184 | tf_op jit(solution)/shard_map/qd,kd->qk/dot_general | solution.py:116
  196.5 11.7 %fusion.4 = (f32[512]{0:T(512)S(1)}, f32[512]{0:T(512)S(1)}, f32[512]{0:T(512)S(1)}, f32[512]{0:T(512)S(1)}) fusion(f32[512,4352]{1,0:T(8,128)S(1)} %get-tuple-element.36, f32[512]{0:T(512)S(1)} %get-tuple-element.35, s32[512]{0:T(512)S(1)} %convert_reduce_fusion.2, s32[4352]{0:T(1024)S(1)} %get-tuple-element.11, s32[512]{0:T(512)S(1)} %iota_add_fusion.2, ...), kind=kLoop, calls=%fused_computation.15 | loop fusion | flops 40105984 | bytes 35741696 | tf_op jit(solution)/shard_map/reduce_sum | solution.py:120
  208.2 7.0 %fusion.57 = f32[512,256]{0,1:T(8,128)} fusion(bf16[8704,512]{1,0:T(8,128)(2,1)S(1)} %bitcast.55, f32[512,4352]{1,0:T(8,128)} %get-tuple-element.40, f32[512]{0:T(512)S(1)} %get-tuple-element.39, f32[512]{0:T(512)S(1)} %get-tuple-element.15, s32[4352]{0:T(1024)S(1)} %get-tuple-element.12, s32[4352]{0:T(1024)S(1)} %get-tuple-element.43, ...), kind=kOutput, calls=%fused_computation.48 | convolution fusion | flops 1154351104 | bytes 11714560 | tf_op jit(solution)/shard_map/dot_general | solution.py:121
  215.3 6.0 %fusion.42 = f32[512,256]{0,1:T(8,128)S(1)} fusion(bf16[8704,512]{1,0:T(8,128)(2,1)S(1)} %bitcast.56, f32[512,4352]{1,0:T(8,128)} %get-tuple-element.34, f32[512]{0:T(512)S(1)} %get-tuple-element.33, f32[512]{0:T(512)S(1)} %get-tuple-element.18, s32[4352]{0:T(1024)S(1)} %get-tuple-element.12, s32[4352]{0:T(1024)S(1)} %get-tuple-element.43, ...), kind=kOutput, calls=%fused_computation.45 | convolution fusion | flops 1154351104 | bytes 11714560 | tf_op jit(solution)/shard_map/dot_general | solution.py:121
  221.3 3.6 %fusion.81 = f32[512,256]{0,1:T(8,128)} fusion(f32[512,256]{0,1:T(8,128)S(1)} %fusion.42, bf16[8704,512]{1,0:T(8,128)(2,1)S(1)} %bitcast.57, f32[512,4352]{1,0:T(8,128)S(1)} %get-tuple-element.38, f32[512]{0:T(512)S(1)} %get-tuple-element.37, f32[512]{0:T(512)S(1)} %get-tuple-element.16, f32[512]{0:T(512)S(1)} %get-tuple-element.17, ...), kind=kOutput, calls=%fused_computation.58 | convolution fusion | flops 1154613248 | bytes 12240896 | tf_op jit(solution)/shard_map/dot_general | solution.py:121
  224.9 4.8 %multiply_reduce_fusion = (f32[512]{0:T(512)S(1)}, f32[512,256]{0,1:T(8,128)S(1)}) fusion(f32[512,256]{0,1:T(8,128)} %fusion.81, f32[512]{0:T(512)S(1)} %get-tuple-element.13, f32[512,256]{0,1:T(8,128)} %fusion.57, f32[512]{0:T(512)S(1)} %get-tuple-element.14, bf16[8704,512]{1,0:T(8,128)(2,1)S(1)} %bitcast.58, f32[512,4352]{1,0:T(8,128)S(1)} %get-tuple-element.36, ...), kind=kOutput, calls=%fused_computation.62 | convolution fusion | flops 1155137024 | bytes 12767236 | tf_op jit(solution)/shard_map/dot_general | solution.py:121
  230.7 1.0 collective-permute-done.3
  231.7 1.7 convolution_convert_fusion
  234.2 66.1 %all-reduce.2.cloned.1.call-done = bf16[256,2048]{1,0:T(8,128)(2,1)} async-done(((bf16[256,2048]{1,0:T(8,128)(2,1)}), bf16[256,2048]{1,0:T(8,128)(2,1)}) %all-reduce.2.cloned.1.call-update) | async-done | bytes 1048592 | tf_op jit(solution)/shard_map/psum | solution.py:153
  300.3 2.6 fusion.27
  (64 shorter events, 9.2 us)
Async XLA Ops:
  7.2 224.5 %copy-start = (bf16[512,2048]{1,0:T(8,128)(2,1)S(1)}, bf16[512,2048]{1,0:T(8,128)(2,1)}, u32[]{:S(2)}) copy-start(bf16[512,2048]{1,0:T(8,128)(2,1)} %param.14) | copy-start | bytes 6291460
  7.2 161.3 %all-gather.2.cloned.1.call-start = ((), (), s32[]{:S(2)}) async-start(), calls=%async_computation | async-start | bytes 17825792 | tf_op jit(solution)/shard_map/all_gather | solution.py:84
  14.2 0.7 copy-start.6
  15.6 35.1 %copy-start.2 = (bf16[256,2048]{1,0:T(8,128)(2,1)S(1)}, bf16[256,2048]{1,0:T(8,128)(2,1)}, u32[]{:S(2)}) copy-start(bf16[256,2048]{1,0:T(8,128)(2,1)} %param.9) | copy-start | bytes 3145732
  16.3 38.9 %copy-start.4 = (bf16[256,2,2,128]{3,2,1,0:T(2,128)(2,1)}, bf16[256,2,2,128]{3,2,1,0:T(2,128)(2,1)S(1)}, u32[]{:S(2)}) copy-start(bf16[256,2,2,128]{3,2,1,0:T(2,128)(2,1)S(1)} %maximum_convert_fusion) | copy-start | bytes 786436
  21.2 37.6 %copy-start.9 = (f32[4,2,128]{2,1,0:T(2,128)S(1)}, f32[4,2,128]{2,1,0:T(2,128)}, u32[]{:S(2)}) copy-start(f32[4,2,128]{2,1,0:T(2,128)} %param.15) | copy-start | bytes 12292
  21.2 37.9 %copy-start.10 = (f32[2,256]{1,0:T(2,128)S(1)}, f32[2,256]{1,0:T(2,128)}, u32[]{:S(2)}) copy-start(f32[2,256]{1,0:T(2,128)} %param.16) | copy-start | bytes 6148
  26.9 5.1 %collective-permute-start.1 = (bf16[256,512]{1,0:T(8,128)(2,1)}, bf16[256,512]{1,0:T(8,128)(2,1)}, u32[]{:S(2)}, u32[]{:S(2)}) collective-permute-start(bf16[256,512]{1,0:T(8,128)(2,1)} %pad_maximum_fusion), channel_id=1, source_target_pairs={{0,4},{4,0},{1,5},{5,1},{2,6},{6,2},{3,7},{7,3},{8,12},{12,8},{9,1... | collective-permute-start | bytes 786440 | tf_op jit(solution)/shard_map/ppermute | solution.py:39
  34.0 13.9 %collective-permute-start.2 = (bf16[512,512]{1,0:T(8,128)(2,1)}, bf16[512,512]{1,0:T(8,128)(2,1)}, u32[]{:S(2)}, u32[]{:S(2)}) collective-permute-start(bf16[512,512]{1,0:T(8,128)(2,1)} %maximum_select_fusion.1), channel_id=1, source_target_pairs={{0,32},{32,0},{1,33},{33,1},{2,34},{34,2},{3,35},{35,3},{4,36},{36... | collective-permute-start | bytes 1572872 | tf_op jit(solution)/shard_map/ppermute | solution.py:82
  50.7 249.6 %all-reduce.2.cloned.1.call-start = ((), (), s32[]{:S(2)}) async-start(), calls=%async_computation.1 | async-start | bytes 2097152 | tf_op jit(solution)/shard_map/psum | solution.py:153
  57.7 2.2 collective-permute-start
  60.0 119.2 %copy-start.7 = (bf16[512,2,128]{2,0,1:T(8,128)(2,1)}, bf16[512,2,128]{2,0,1:T(8,128)(2,1)S(1)}, u32[]{:S(2)}) copy-start(bf16[512,2,128]{2,0,1:T(8,128)(2,1)S(1)} %maximum_select_fusion.2) | copy-start | bytes 786436
  179.2 4.0 %copy-start.1 = (bf16[17,512,512]{2,1,0:T(8,128)(2,1)S(1)}, bf16[17,512,512]{2,1,0:T(8,128)(2,1)}, u32[]{:S(2)}) copy-start(bf16[17,512,512]{2,1,0:T(8,128)(2,1)} %gather_fusion) | copy-start | bytes 26738692
  183.2 3.6 %copy-start.8 = (bf16[512,2,128]{2,0,1:T(8,128)(2,1)S(1)}, bf16[512,2,128]{2,0,1:T(8,128)(2,1)}, u32[]{:S(2)}) copy-start(bf16[512,2,128]{2,0,1:T(8,128)(2,1)} %copy-done.7) | copy-start | bytes 786436
  224.9 8.5 %copy-start.5 = (bf16[256,2,2,128]{3,2,1,0:T(2,128)(2,1)S(1)}, bf16[256,2,2,128]{3,2,1,0:T(2,128)(2,1)}, u32[]{:S(2)}) copy-start(bf16[256,2,2,128]{3,2,1,0:T(2,128)(2,1)} %copy-done.4) | copy-start | bytes 786436
  224.9 75.4 %copy-start.3 = (bf16[256,2048]{1,0:T(8,128)(2,1)S(1)}, bf16[256,2048]{1,0:T(8,128)(2,1)}, u32[]{:S(2)}) copy-start(bf16[256,2048]{1,0:T(8,128)(2,1)} %param.9) | copy-start | bytes 3145732
  229.9 1.8 collective-permute-start.3
Sparse Core Ops, SparseCore 0:
  50.8 117.6 all-gather.1
  233.5 66.7 all-reduce.1

commit v2 on v1

--- a/solution.py
+++ b/solution.py
@@ -73,14 +73,17 @@
         v_h = lax.dynamic_index_in_dim(values.reshape(rows, heads, VD), h, axis=1, keepdims=False)
         return jnp.concatenate([k_h, v_h], axis=1)
 
-    def in_order(mine, theirs):
-        return jnp.where(core == 0, jnp.concatenate([mine, theirs], axis=0), jnp.concatenate([theirs, mine], axis=0))
+    def in_order(mine, theirs, first_is_mine):
+        rows_each = mine.shape[0]
+        both = jnp.zeros((2 * rows_each,) + mine.shape[1:], mine.dtype)
+        both = lax.dynamic_update_slice_in_dim(both, mine, jnp.where(first_is_mine, 0, rows_each), axis=0)
+        return lax.dynamic_update_slice_in_dim(both, theirs, jnp.where(first_is_mine, rows_each, 0), axis=0)
 
     span = 2 * rows
-    kv_pair = in_order(head_kv(core), swap_cores(head_kv(1 - core)))
+    kv_pair = in_order(head_kv(core), swap_cores(head_kv(1 - core)), core == 0)
     z = lax.axis_index("z")
     kv_z = lax.ppermute(kv_pair, "z", [(0, 1), (1, 0)])
-    kv_quad = jnp.where(z == 0, jnp.concatenate([kv_pair, kv_z], axis=0), jnp.concatenate([kv_z, kv_pair], axis=0))
+    kv_quad = in_order(kv_pair, kv_z, z == 0)
     gathered = lax.all_gather(kv_quad, ("y", "x"), axis=0, tiled=True)
     query = rotate(
         jnp.dot(normed, w_query, preferred_element_type=jnp.float32).reshape(rows, heads, 2, QK),
@@ -89,6 +92,7 @@
     q_pair = in_order(
         lax.dynamic_index_in_dim(query, core, axis=1, keepdims=False),
         swap_cores(lax.dynamic_index_in_dim(query, 1 - core, axis=1, keepdims=False)),
+        core == 0,
     )
 
     reach = min(MAXLEN // span + 1, chips)
@@ -101,40 +105,38 @@
     kv_window = jnp.take(gathered.reshape(chips, span, -1), slot, axis=0, mode="clip").reshape(window, -1)
     q_index = base + jnp.arange(span, dtype=jnp.int32)
     q_seg, unused = locate(q_index, lengths)
-    pieces = 2
+    pieces = 4
     piece = window // pieces
 
-    def part(p):
+    def absorb(p, carry):
         key_index = start + p * piece + jnp.arange(piece, dtype=jnp.int32)
         k_seg, unused = locate(key_index, lengths)
         allowed = (key_index[None, :] <= q_index[:, None]) & (k_seg[None, :] == q_seg[:, None])
-        kv_win = kv_window[p * piece : (p + 1) * piece]
+        kv_win = lax.dynamic_slice_in_dim(kv_window, p * piece, piece, axis=0)
         v_win = kv_win[:, 2 * QK :]
-        stats = []
+        updated = []
         for m in range(2):
+            top, mass, acc = carry[m]
             k_m = kv_win[:, m * QK : (m + 1) * QK]
             scores = jnp.einsum("qd,kd->qk", q_pair[:, m, :], k_m, preferred_element_type=jnp.float32) * scale
             scores = jnp.where(allowed, scores, masked_score)
-            top = jnp.max(scores, axis=-1, keepdims=True)
-            weights = jnp.where(allowed, jnp.exp(scores - top), 0.0)
-            mass = jnp.sum(weights, axis=-1, keepdims=True)
-            acc = jnp.dot(weights.astype(jnp.bfloat16), v_win, preferred_element_type=jnp.float32)
-            stats.append((top, mass, acc))
-        return stats
+            new_top = jnp.maximum(top, jnp.max(scores, axis=-1, keepdims=True))
+            weights = jnp.where(allowed, jnp.exp(scores - new_top), 0.0)
+            fade = jnp.exp(top - new_top)
+            mass = mass * fade + jnp.sum(weights, axis=-1, keepdims=True)
+            acc = acc * fade + jnp.dot(weights.astype(jnp.bfloat16), v_win, preferred_element_type=jnp.float32)
+            updated.append((new_top, mass, acc))
+        return tuple(updated)
 
-    all_stats = [part(p) for p in range(pieces)]
+    empty = (
+        jnp.full((span, 1), masked_score, jnp.float32),
+        jnp.zeros((span, 1), jnp.float32),
+        jnp.zeros((span, VD), jnp.float32),
+    )
+    final = lax.fori_loop(0, pieces, absorb, (empty, empty))
 
     def attend(m):
-        tops = [stats[m][0] for stats in all_stats]
-        top = tops[0]
-        for other in tops[1:]:
-            top = jnp.maximum(top, other)
-        acc = 0.0
-        mass = 0.0
-        for stats in all_stats:
-            fade = jnp.exp(stats[m][0] - top)
-            mass = mass + stats[m][1] * fade
-            acc = acc + stats[m][2] * fade
+        top, mass, acc = final[m]
         return acc / mass
 
     lam_h = lax.dynamic_index_in_dim(lam, core, keepdims=False)

time: 310 us -> 333 us (1.074)
  matrix products: 49.6 us -> 69.1 us
  local copies, waits for them, and re-layouts: 22.1 us -> 31.4 us
  other arithmetic: 29.1 us -> 25.3 us
    dot_general x8 -> x16, matrix products: 38.7 us -> 58.9 us  [the longest x8 33.4 us: absorb(): jnp.dot(weights.astype(jnp.bfloat16), v_win, preferred_element_type=jnp.f...]
    dynamic_update_slice x0 -> x5, local copies, waits for them, and re-layouts: none -> 5.46 us  [the longest x3 3.55 us: in_order(): lax.dynamic_update_slice_in_dim(both, theirs, jnp.where(first_is_mine, ro...]
    select_n x3 -> x0, other arithmetic: 4.81 us -> none  [the longest x1 2.78 us: on_device(): jnp.where(z == 0, jnp.concatenate([kv_pair, kv_z], axis=0), jnp.concatena...]
    while x0 -> x64, local copies, waits for them, and re-layouts: none -> 3.52 us
    reduce_sum x1 -> x5, other arithmetic: 11.7 us -> 11.7 us  [the longest x4 9.5 us: absorb(): mass = mass * fade + jnp.sum(weights, axis=-1, keepdims=True)]
  transfers between devices with their start and end apart: 6 -> 6, of which waited for: 4 -> 4; matrix products, arithmetic and copies ran while one was open for 3% -> 5% of each run, Pallas kernels for 0% -> 0%
where the time goes in v2:
time: 333 us; the launch traced here: 332 us
  waiting for transfers between devices  186 us (56%)
  matrix products  69.1 us (21%)
  local copies, waits for them, and re-layouts  31.4 us (9%)
  other arithmetic  25.3 us (8%)
  between operations  14.4 us (4%)
  starting transfers between devices  5.17 us (2%)
    all_gather x1, waiting for transfers between devices, on_device(): gathered = lax.all_gather(kv_quad, ('y', 'x'), axis=0, tiled=True)  108 us
    psum x1, waiting for transfers between devices, on_device(): lax.psum(jnp.dot(merged, w_out, preferred_element_type=jnp.float32).astyp...  66.2 us
    dot_general x8, matrix products, absorb(): jnp.dot(weights.astype(jnp.bfloat16), v_win, preferred_element_type=jnp.f...  33.4 us
    dot_general x8, matrix products, absorb(): jnp.einsum('qd,kd->qk', q_pair[:, m, :], k_m, preferred_element_type=jnp....  25.5 us
    ppermute x1, waiting for transfers between devices, on_device(): kv_z = lax.ppermute(kv_pair, 'z', [(0, 1), (1, 0)])  11 us
    gather x1, local copies, waits for them, and re-layouts, on_device(): jnp.take(gathered.reshape(chips, span, -1), slot, axis=0, mode='clip')  10.7 us
    reduce_sum x4, other arithmetic, absorb(): mass = mass * fade + jnp.sum(weights, axis=-1, keepdims=True)  9.5 us
  transfers between devices with their start and end apart: 6, of which 4 were waited for; matrix products, arithmetic and copies ran while one was open for 5% of the time, Pallas kernels for 0%

profile of v2, /device:TPU:1, one launch (start us, length us, event | category | flops | bytes accessed | tf_op | source)
XLA Modules:
  0.0 331.9 jit_solution(6741299401820924802)
XLA Ops:
  10.6 2.7 fusion.63
  13.7 2.7 convolution_convert_fusion.1
  20.7 2.4 constant_dynamic-slice_fusion.3
  23.8 3.2 collective-permute-start
  35.1 11.0 %collective-permute-done.1 = bf16[512,512]{1,0:T(8,128)(2,1)} collective-permute-done((bf16[512,512]{1,0:T(8,128)(2,1)}, bf16[512,512]{1,0:T(8,128)(2,1)}, u32[]{:S(2)}, u32[]{:S(2)}) %collective-permute-start.1) | collective-permute-done | bytes 524320 | tf_op jit(solution)/shard_map/ppermute | solution.py:85
  48.0 3.2 fusion.60
  58.0 107.8 %all-gather.2.cloned.1.call-done = bf16[16384,512]{1,0:T(8,128)(2,1)} async-done(((bf16[1024,512]{1,0:T(8,128)(2,1)}), bf16[16384,512]{1,0:T(8,128)(2,1)}) %all-gather.2.cloned.1.call-update) | async-done | bytes 16777232 | tf_op jit(solution)/shard_map/all_gather | solution.py:87
  165.8 10.7 %gather_fusion = bf16[17,512,512]{2,1,0:T(8,128)(2,1)} fusion(bf16[32,512,512]{2,1,0:T(8,128)(2,1)} %bitcast.91, s32[1024]{0:T(1024)S(1)} %pad_clamp_fusion), kind=kCustom, calls=%fused_computation | custom fusion | bytes 17825860 | tf_op jit(solution)/shard_map/jit(_take)/gather | solution.py:105
  176.5 73.1 %while.26 = (s32[]{:T(128)}, f32[512,1]{0,1:T(1,128)S(1)}, f32[512,1]{0,1:T(1,128)S(1)}, f32[512,256]{1,0:T(8,128)}, f32[512,1]{0,1:T(1,128)S(1)}, /*index=5*/f3...) while((s32[]{:T(128)}, f32[512,1]{0,1:T(1,128)S(1)}, ...), condition=%wide.region_12.13_spmd.clone, body=%wide.region_6.12_spmd.clone.sunk | while | flops 1748859904 | bytes 81415152 | solution.py:136
  176.6 3.7 %fusion.87 = (f32[512]{0:T(512)S(1)}, f32[512,2176]{0,1:T(8,128)}) fusion(bf16[512,2,128]{2,0,1:T(8,128)(2,1)S(1)} %get-tuple-element.555, bf16[8704,512]{1,0:T(8,128)(2,1)} %get-tuple-element.554, s32[]{:T(128)S(6)} %select_n.222, s32[512]{0:T(512)S(1)} %get-tuple-element.553, s32[2176]{0:T(1024)S(1)} %convert_reduce_fusion.4, ...), kind=kOutput, calls=%fused_computation.138.clone.1 | convolution fusion | flops 291896832 | bytes 5175300 | tf_op jit(solution)/shard_map/while/body/eval_jaxpr/qd,kd->qk/dot_general | solution.py:121
  180.4 2.6 fusion.89
  183.1 2.4 fusion.91
  185.5 5.4 %fusion.94 = f32[512,256]{1,0:T(8,128)} fusion(f32[512,2176]{0,1:T(8,128)} %copy-done.1, f32[512]{0:T(512)S(1)} %bitcast.95, bf16[8704,512]{1,0:T(8,128)(2,1)} %get-tuple-element.554, s32[]{:T(128)S(6)} %select_n.222, s32[]{:T(128)S(6)} %add.404, f32[512,256]{1,0:T(8,128)} %get-tuple-element.531, f32[512]{0:T(512)S(1)} %bitcast.108, ...), kind=kOutput, calls=%fused_computation.22.clone.1 | convolution fusion | flops 577503232 | bytes 6644745 | tf_op jit(solution)/shard_map/while/body/eval_jaxpr/dot_general | solution.py:127
  190.9 2.9 fusion.93
  194.8 3.8 %fusion.87 = (f32[512]{0:T(512)S(1)}, f32[512,2176]{0,1:T(8,128)}) fusion(bf16[512,2,128]{2,0,1:T(8,128)(2,1)S(1)} %get-tuple-element.555, bf16[8704,512]{1,0:T(8,128)(2,1)} %get-tuple-element.554, s32[]{:T(128)S(6)} %select_n.222, s32[512]{0:T(512)S(1)} %get-tuple-element.553, s32[2176]{0:T(1024)S(1)} %convert_reduce_fusion.4, ...), kind=kOutput, calls=%fused_computation.138.clone.1 | convolution fusion | flops 291896832 | bytes 5175300 | tf_op jit(solution)/shard_map/while/body/eval_jaxpr/qd,kd->qk/dot_general | solution.py:121
  198.5 2.6 fusion.89
  201.2 2.4 fusion.91
  203.7 5.5 %fusion.94 = f32[512,256]{1,0:T(8,128)} fusion(f32[512,2176]{0,1:T(8,128)} %copy-done.1, f32[512]{0:T(512)S(1)} %bitcast.95, bf16[8704,512]{1,0:T(8,128)(2,1)} %get-tuple-element.554, s32[]{:T(128)S(6)} %select_n.222, s32[]{:T(128)S(6)} %add.404, f32[512,256]{1,0:T(8,128)} %get-tuple-element.531, f32[512]{0:T(512)S(1)} %bitcast.108, ...), kind=kOutput, calls=%fused_computation.22.clone.1 | convolution fusion | flops 577503232 | bytes 6644745 | tf_op jit(solution)/shard_map/while/body/eval_jaxpr/dot_general | solution.py:127
  209.2 2.9 fusion.93
  213.1 3.8 %fusion.87 = (f32[512]{0:T(512)S(1)}, f32[512,2176]{0,1:T(8,128)}) fusion(bf16[512,2,128]{2,0,1:T(8,128)(2,1)S(1)} %get-tuple-element.555, bf16[8704,512]{1,0:T(8,128)(2,1)} %get-tuple-element.554, s32[]{:T(128)S(6)} %select_n.222, s32[512]{0:T(512)S(1)} %get-tuple-element.553, s32[2176]{0:T(1024)S(1)} %convert_reduce_fusion.4, ...), kind=kOutput, calls=%fused_computation.138.clone.1 | convolution fusion | flops 291896832 | bytes 5175300 | tf_op jit(solution)/shard_map/while/body/eval_jaxpr/qd,kd->qk/dot_general | solution.py:121
  216.8 2.6 fusion.89
  219.5 2.4 fusion.91
  222.0 5.5 %fusion.94 = f32[512,256]{1,0:T(8,128)} fusion(f32[512,2176]{0,1:T(8,128)} %copy-done.1, f32[512]{0:T(512)S(1)} %bitcast.95, bf16[8704,512]{1,0:T(8,128)(2,1)} %get-tuple-element.554, s32[]{:T(128)S(6)} %select_n.222, s32[]{:T(128)S(6)} %add.404, f32[512,256]{1,0:T(8,128)} %get-tuple-element.531, f32[512]{0:T(512)S(1)} %bitcast.108, ...), kind=kOutput, calls=%fused_computation.22.clone.1 | convolution fusion | flops 577503232 | bytes 6644745 | tf_op jit(solution)/shard_map/while/body/eval_jaxpr/dot_general | solution.py:127
  227.5 2.9 fusion.93
  231.4 3.8 %fusion.87 = (f32[512]{0:T(512)S(1)}, f32[512,2176]{0,1:T(8,128)}) fusion(bf16[512,2,128]{2,0,1:T(8,128)(2,1)S(1)} %get-tuple-element.555, bf16[8704,512]{1,0:T(8,128)(2,1)} %get-tuple-element.554, s32[]{:T(128)S(6)} %select_n.222, s32[512]{0:T(512)S(1)} %get-tuple-element.553, s32[2176]{0:T(1024)S(1)} %convert_reduce_fusion.4, ...), kind=kOutput, calls=%fused_computation.138.clone.1 | convolution fusion | flops 291896832 | bytes 5175300 | tf_op jit(solution)/shard_map/while/body/eval_jaxpr/qd,kd->qk/dot_general | solution.py:121
  235.1 2.6 fusion.89
  237.8 2.4 fusion.91
  240.3 5.5 %fusion.94 = f32[512,256]{1,0:T(8,128)} fusion(f32[512,2176]{0,1:T(8,128)} %copy-done.1, f32[512]{0:T(512)S(1)} %bitcast.95, bf16[8704,512]{1,0:T(8,128)(2,1)} %get-tuple-element.554, s32[]{:T(128)S(6)} %select_n.222, s32[]{:T(128)S(6)} %add.404, f32[512,256]{1,0:T(8,128)} %get-tuple-element.531, f32[512]{0:T(512)S(1)} %bitcast.108, ...), kind=kOutput, calls=%fused_computation.22.clone.1 | convolution fusion | flops 577503232 | bytes 6644745 | tf_op jit(solution)/shard_map/while/body/eval_jaxpr/dot_general | solution.py:127
  245.8 2.9 fusion.93
  249.6 2.2 multiply_reduce_fusion
  256.2 66.2 %all-reduce.2.cloned.1.call-done = bf16[256,2048]{1,0:T(8,128)(2,1)} async-done(((bf16[256,2048]{1,0:T(8,128)(2,1)}), bf16[256,2048]{1,0:T(8,128)(2,1)}) %all-reduce.2.cloned.1.call-update) | async-done | bytes 1048592 | tf_op jit(solution)/shard_map/psum | solution.py:155
  322.5 2.6 fusion.44
  (175 shorter events, 34.0 us)
Async XLA Ops:
  7.2 246.6 %copy-start = (bf16[512,2048]{1,0:T(8,128)(2,1)S(1)}, bf16[512,2048]{1,0:T(8,128)(2,1)}, u32[]{:S(2)}) copy-start(bf16[512,2048]{1,0:T(8,128)(2,1)} %param.16) | copy-start | bytes 6291460
  7.2 6.5 %copy-start.10 = (f32[2048]{0:T(1024)S(1)}, f32[2048]{0:T(1024)}, u32[]{:S(2)}) copy-start(f32[2048]{0:T(1024)} %param.12) | copy-start | bytes 24580
  7.2 158.6 %all-gather.2.cloned.1.call-start = ((), (), s32[]{:S(2)}) async-start(), calls=%async_computation | async-start | bytes 17825792 | tf_op jit(solution)/shard_map/all_gather | solution.py:87
  20.7 27.3 %copy-start.2 = (bf16[256,2048]{1,0:T(8,128)(2,1)S(1)}, bf16[256,2048]{1,0:T(8,128)(2,1)}, u32[]{:S(2)}) copy-start(bf16[256,2048]{1,0:T(8,128)(2,1)} %param.11) | copy-start | bytes 3145732
  23.8 6.7 %collective-permute-start = (bf16[256,512]{1,0:T(8,128)(2,1)}, bf16[256,512]{1,0:T(8,128)(2,1)}, u32[]{:S(2)}, u32[]{:S(2)}) collective-permute-start(bf16[256,512]{1,0:T(8,128)(2,1)} %pad_maximum_fusion), channel_id=1, source_target_pairs={{0,4},{4,0},{1,5},{5,1},{2,6},{6,2},{3,7},{7,3},{8,12},{12,8},{9,1... | collective-permute-start | bytes 786440 | tf_op jit(solution)/shard_map/ppermute | solution.py:39
  32.2 13.9 %collective-permute-start.1 = (bf16[512,512]{1,0:T(8,128)(2,1)}, bf16[512,512]{1,0:T(8,128)(2,1)}, u32[]{:S(2)}, u32[]{:S(2)}) collective-permute-start(bf16[512,512]{1,0:T(8,128)(2,1)} %constant_dynamic-update-slice_fusion.3), channel_id=1, source_target_pairs={{0,32},{32,0},{1,33},{33,1},{2,34},{34,2},{3,35},{35,3},{4,36},{36... | collective-permute-start | bytes 1572872 | tf_op jit(solution)/shard_map/ppermute | solution.py:85
  47.9 8.2 %copy-start.8 = (f32[4,2,128]{2,1,0:T(2,128)S(1)}, f32[4,2,128]{2,1,0:T(2,128)}, u32[]{:S(2)}) copy-start(f32[4,2,128]{2,1,0:T(2,128)} %param.17) | copy-start | bytes 12292
  48.0 8.4 %copy-start.9 = (f32[2,256]{1,0:T(2,128)S(1)}, f32[2,256]{1,0:T(2,128)}, u32[]{:S(2)}) copy-start(f32[2,256]{1,0:T(2,128)} %param.18) | copy-start | bytes 6148
  48.0 274.5 %all-reduce.2.cloned.1.call-start = ((), (), s32[]{:S(2)}) async-start(), calls=%async_computation.1 | async-start | bytes 2097152 | tf_op jit(solution)/shard_map/psum | solution.py:155
  55.0 3.0 collective-permute-start.2
  180.4 2.7 slice-start
  180.4 2.7 slice-start.1
  183.1 7.8 %slice-start.2 = ((s8[4456448]{0:T(1024)(128)(4,1)}), s8[262144]{0:T(1024)(128)(4,1)S(1)}, s32[]{:S(2)}) async-start(s8[4456448]{0:T(1024)(128)(4,1)} %bitcast.88), calls=%async_computation.4 | async-start | bytes 524288 | tf_op jit(solution)/shard_map/while
  185.5 5.4 %slice-start.3 = ((s8[4456448]{0:T(1024)(128)(4,1)}), s8[4194304]{0:T(1024)(128)(4,1)S(1)}, s32[]{:S(2)}) async-start(s8[4456448]{0:T(1024)(128)(4,1)} %bitcast.88), calls=%async_computation.5 | async-start | bytes 8388608 | tf_op jit(solution)/shard_map/while
  185.5 5.4 %copy-start.5 = (f32[512,256]{1,0:T(8,128)S(1)}, f32[512,256]{1,0:T(8,128)}, u32[]{:S(2)}) copy-start(f32[512,256]{1,0:T(8,128)} %get-tuple-element.528) | copy-start | bytes 1572868 | tf_op jit(solution)/shard_map/while
  198.5 2.7 slice-start
  198.5 2.7 slice-start.1
  201.2 8.0 %slice-start.2 = ((s8[4456448]{0:T(1024)(128)(4,1)}), s8[262144]{0:T(1024)(128)(4,1)S(1)}, s32[]{:S(2)}) async-start(s8[4456448]{0:T(1024)(128)(4,1)} %bitcast.88), calls=%async_computation.4 | async-start | bytes 524288 | tf_op jit(solution)/shard_map/while
  203.7 5.6 %slice-start.3 = ((s8[4456448]{0:T(1024)(128)(4,1)}), s8[4194304]{0:T(1024)(128)(4,1)S(1)}, s32[]{:S(2)}) async-start(s8[4456448]{0:T(1024)(128)(4,1)} %bitcast.88), calls=%async_computation.5 | async-start | bytes 8388608 | tf_op jit(solution)/shard_map/while
  203.7 5.5 %copy-start.5 = (f32[512,256]{1,0:T(8,128)S(1)}, f32[512,256]{1,0:T(8,128)}, u32[]{:S(2)}) copy-start(f32[512,256]{1,0:T(8,128)} %get-tuple-element.528) | copy-start | bytes 1572868 | tf_op jit(solution)/shard_map/while
  216.8 2.7 slice-start
  216.8 2.7 slice-start.1
  219.5 8.0 %slice-start.2 = ((s8[4456448]{0:T(1024)(128)(4,1)}), s8[262144]{0:T(1024)(128)(4,1)S(1)}, s32[]{:S(2)}) async-start(s8[4456448]{0:T(1024)(128)(4,1)} %bitcast.88), calls=%async_computation.4 | async-start | bytes 524288 | tf_op jit(solution)/shard_map/while
  222.0 5.6 %slice-start.3 = ((s8[4456448]{0:T(1024)(128)(4,1)}), s8[4194304]{0:T(1024)(128)(4,1)S(1)}, s32[]{:S(2)}) async-start(s8[4456448]{0:T(1024)(128)(4,1)} %bitcast.88), calls=%async_computation.5 | async-start | bytes 8388608 | tf_op jit(solution)/shard_map/while
  222.0 5.5 %copy-start.5 = (f32[512,256]{1,0:T(8,128)S(1)}, f32[512,256]{1,0:T(8,128)}, u32[]{:S(2)}) copy-start(f32[512,256]{1,0:T(8,128)} %get-tuple-element.528) | copy-start | bytes 1572868 | tf_op jit(solution)/shard_map/while
  235.1 2.7 slice-start
  235.1 2.7 slice-start.1
  237.8 8.0 %slice-start.2 = ((s8[4456448]{0:T(1024)(128)(4,1)}), s8[262144]{0:T(1024)(128)(4,1)S(1)}, s32[]{:S(2)}) async-start(s8[4456448]{0:T(1024)(128)(4,1)} %bitcast.88), calls=%async_computation.4 | async-start | bytes 524288 | tf_op jit(solution)/shard_map/while
  240.3 5.6 %slice-start.3 = ((s8[4456448]{0:T(1024)(128)(4,1)}), s8[4194304]{0:T(1024)(128)(4,1)S(1)}, s32[]{:S(2)}) async-start(s8[4456448]{0:T(1024)(128)(4,1)} %bitcast.88), calls=%async_computation.5 | async-start | bytes 8388608 | tf_op jit(solution)/shard_map/while
  240.3 5.5 %copy-start.5 = (f32[512,256]{1,0:T(8,128)S(1)}, f32[512,256]{1,0:T(8,128)}, u32[]{:S(2)}) copy-start(f32[512,256]{1,0:T(8,128)} %get-tuple-element.528) | copy-start | bytes 1572868 | tf_op jit(solution)/shard_map/while
  249.6 72.9 %copy-start.3 = (bf16[256,2048]{1,0:T(8,128)(2,1)S(1)}, bf16[256,2048]{1,0:T(8,128)(2,1)}, u32[]{:S(2)}) copy-start(bf16[256,2048]{1,0:T(8,128)(2,1)} %param.11) | copy-start | bytes 3145732
  251.9 1.8 collective-permute-start.3
  (10 other events, 15.5 us)
Sparse Core Ops, SparseCore 0:
  48.1 117.6 all-gather.1
  255.6 66.8 all-reduce.1

commit v3 on v1

--- a/solution.py
+++ b/solution.py
@@ -73,14 +73,17 @@
         v_h = lax.dynamic_index_in_dim(values.reshape(rows, heads, VD), h, axis=1, keepdims=False)
         return jnp.concatenate([k_h, v_h], axis=1)
 
-    def in_order(mine, theirs):
-        return jnp.where(core == 0, jnp.concatenate([mine, theirs], axis=0), jnp.concatenate([theirs, mine], axis=0))
+    def in_order(mine, theirs, first_is_mine):
+        rows_each = mine.shape[0]
+        both = jnp.zeros((2 * rows_each,) + mine.shape[1:], mine.dtype)
+        both = lax.dynamic_update_slice_in_dim(both, mine, jnp.where(first_is_mine, 0, rows_each), axis=0)
+        return lax.dynamic_update_slice_in_dim(both, theirs, jnp.where(first_is_mine, rows_each, 0), axis=0)
 
     span = 2 * rows
-    kv_pair = in_order(head_kv(core), swap_cores(head_kv(1 - core)))
+    kv_pair = in_order(head_kv(core), swap_cores(head_kv(1 - core)), core == 0)
     z = lax.axis_index("z")
     kv_z = lax.ppermute(kv_pair, "z", [(0, 1), (1, 0)])
-    kv_quad = jnp.where(z == 0, jnp.concatenate([kv_pair, kv_z], axis=0), jnp.concatenate([kv_z, kv_pair], axis=0))
+    kv_quad = in_order(kv_pair, kv_z, z == 0)
     gathered = lax.all_gather(kv_quad, ("y", "x"), axis=0, tiled=True)
     query = rotate(
         jnp.dot(normed, w_query, preferred_element_type=jnp.float32).reshape(rows, heads, 2, QK),
@@ -89,6 +92,7 @@
     q_pair = in_order(
         lax.dynamic_index_in_dim(query, core, axis=1, keepdims=False),
         swap_cores(lax.dynamic_index_in_dim(query, 1 - core, axis=1, keepdims=False)),
+        core == 0,
     )
 
     reach = min(MAXLEN // span + 1, chips)

time: 310 us -> 311 us (level)
  local copies, waits for them, and re-layouts: 22.1 us -> 29.4 us
  other arithmetic: 29.1 us -> 25 us
    dynamic_update_slice x0 -> x5, local copies, waits for them, and re-layouts: none -> 5.46 us  [the longest x3 3.55 us: in_order(): lax.dynamic_update_slice_in_dim(both, theirs, jnp.where(first_is_mine, ro...]
    select_n x3 -> x0, other arithmetic: 4.81 us -> none  [the longest x1 2.78 us: on_device(): jnp.where(z == 0, jnp.concatenate([kv_pair, kv_z], axis=0), jnp.concatena...]
  transfers between devices with their start and end apart: 6 -> 6, of which waited for: 4 -> 4; matrix products, arithmetic and copies ran while one was open for 3% -> 5% of each run, Pallas kernels for 0% -> 0%
where the time goes in v3:
time: 311 us; the launch traced here: 310 us
  waiting for transfers between devices  186 us (60%)
  matrix products  49.6 us (16%)
  local copies, waits for them, and re-layouts  29.4 us (9%)
  other arithmetic  25 us (8%)
  between operations  14.4 us (5%)
  starting transfers between devices  5.18 us (2%)
    all_gather x1, waiting for transfers between devices, on_device(): gathered = lax.all_gather(kv_quad, ('y', 'x'), axis=0, tiled=True)  108 us
    psum x1, waiting for transfers between devices, on_device(): lax.psum(jnp.dot(merged, w_out, preferred_element_type=jnp.float32).astyp...  66.1 us
    dot_general x4, matrix products, part(): jnp.dot(weights.astype(jnp.bfloat16), v_win, preferred_element_type=jnp.f...  21.4 us
    dot_general x4, matrix products, part(): jnp.einsum('qd,kd->qk', q_pair[:, m, :], k_m, preferred_element_type=jnp....  17.2 us
    reduce_sum x1, other arithmetic, part(): mass = jnp.sum(weights, axis=-1, keepdims=True)  11.7 us
    ppermute x1, waiting for transfers between devices, on_device(): kv_z = lax.ppermute(kv_pair, 'z', [(0, 1), (1, 0)])  11 us
    gather x1, local copies, waits for them, and re-layouts, on_device(): jnp.take(gathered.reshape(chips, span, -1), slot, axis=0, mode='clip')  10.7 us
  transfers between devices with their start and end apart: 6, of which 4 were waited for; matrix products, arithmetic and copies ran while one was open for 5% of the time, Pallas kernels for 0%

profile of v3, /device:TPU:1, one launch (start us, length us, event | category | flops | bytes accessed | tf_op | source)
XLA Modules:
  0.0 310.0 jit_solution(15787733632800340232)
XLA Ops:
  9.1 1.5 fusion.24
  10.6 2.7 fusion.110
  17.8 3.4 %convolution_convert_fusion.1 = bf16[256,512]{1,0:T(8,128)(2,1)} fusion(bf16[2048,512]{1,0:T(8,128)(2,1)} %param.13, bf16[256,2048]{1,0:T(8,128)(2,1)} %param.9, f32[2048]{0:T(1024)} %param.10, f32[256]{0:T(256)S(1)} %add_rsqrt_fusion.1), kind=kOutput, calls=%fused_computation.49 | convolution fusion | flops 539099136 | bytes 3417088 | tf_op jit(solution)/shard_map/dot_general | solution.py:62
  21.2 1.7 reshape.382
  23.0 2.3 constant_dynamic-slice_fusion.3
  25.3 1.6 pad_maximum_fusion
  26.9 3.2 %collective-permute-start.1 = (bf16[256,512]{1,0:T(8,128)(2,1)}, bf16[256,512]{1,0:T(8,128)(2,1)}, u32[]{:S(2)}, u32[]{:S(2)}) collective-permute-start(bf16[256,512]{1,0:T(8,128)(2,1)} %pad_maximum_fusion), channel_id=1, source_target_pairs={{0,4},{4,0},{1,5},{5,1},{2,6},{6,2},{3,7},{7,3},{8,12},{12,8},{9,1... | collective-permute-start | bytes 786440 | tf_op jit(solution)/shard_map/ppermute | solution.py:39
  31.1 1.0 copy.33
  33.6 1.7 constant_dynamic-update-slice_fusion.2
  35.3 1.0 broadcast_in_dim.35
  36.3 1.9 constant_dynamic-update-slice_fusion.1
  38.2 11.0 %collective-permute-done.2 = bf16[512,512]{1,0:T(8,128)(2,1)} collective-permute-done((bf16[512,512]{1,0:T(8,128)(2,1)}, bf16[512,512]{1,0:T(8,128)(2,1)}, u32[]{:S(2)}, u32[]{:S(2)}) %collective-permute-start.2) | collective-permute-done | bytes 524320 | tf_op jit(solution)/shard_map/ppermute | solution.py:85
  49.1 1.9 constant_dynamic-update-slice_fusion
  51.1 3.2 %fusion.112 = f32[256,512]{1,0:T(8,128)} fusion(bf16[2048,512]{1,0:T(8,128)(2,1)} %param.11, bf16[256,2048]{1,0:T(8,128)(2,1)S(1)} %copy-done.2, f32[2048]{0:T(1024)} %param.10, f32[256]{0:T(256)S(1)} %add_rsqrt_fusion.1), kind=kOutput, calls=%fused_computation.154 | convolution fusion | flops 538968064 | bytes 3679232 | tf_op jit(solution)/shard_map/dot_general | solution.py:89
  54.2 1.4 reshape.379
  55.6 1.7 add_convert_fusion
  58.1 1.1 collective-permute-start
  60.4 108.4 %all-gather.2.cloned.1.call-done = bf16[16384,512]{1,0:T(8,128)(2,1)} async-done(((bf16[1024,512]{1,0:T(8,128)(2,1)}), bf16[16384,512]{1,0:T(8,128)(2,1)}) %all-gather.2.cloned.1.call-update) | async-done | bytes 16777232 | tf_op jit(solution)/shard_map/all_gather | solution.py:87
  168.8 10.7 %gather_fusion = bf16[17,512,512]{2,1,0:T(8,128)(2,1)} fusion(bf16[32,512,512]{2,1,0:T(8,128)(2,1)} %bitcast.58, s32[1024]{0:T(1024)S(1)} %pad_clamp_fusion), kind=kCustom, calls=%fused_computation | custom fusion | bytes 17825860 | tf_op jit(solution)/shard_map/jit(_take)/gather | solution.py:105
  179.6 3.9 %fusion.119 = (f32[512]{0:T(512)S(1)}, f32[512,4352]{1,0:T(8,128)S(1)}) fusion(bf16[8704,512]{1,0:T(8,128)(2,1)} %bitcast.50, bf16[512,2,128]{2,0,1:T(8,128)(2,1)S(1)} %constant_dynamic-update-slice_fusion.3, s32[512]{0:T(512)S(1)} %convert_reduce_fusion.2, s32[4352]{0:T(1024)S(1)} %get-tuple-element.11, s32[512]{0:T(512)S(1)} %iota_add_fusion.2, ...), kind=kOutput, calls=%fused_computation.156 | convolution fusion | flops 583794176 | bytes 10205184 | tf_op jit(solution)/shard_map/qd,kd->qk/dot_general | solution.py:120
  183.5 3.6 %fusion.120 = (f32[512]{0:T(512)S(1)}, f32[512,4352]{1,0:T(8,128)S(1)}) fusion(bf16[8704,512]{1,0:T(8,128)(2,1)S(1)} %bitcast.51, bf16[512,2,128]{2,0,1:T(8,128)(2,1)} %copy-done.7, s32[512]{0:T(512)S(1)} %convert_reduce_fusion.2, s32[4352]{0:T(1024)S(1)} %get-tuple-element.11, s32[512]{0:T(512)S(1)} %iota_add_fusion.2, s32[4352]{0:T(1024)S(1)} %iota_add_fusion.1), kind=kOutput, calls=%fused_computation.157 | convolution fusion | flops 583794176 | bytes 10205184 | tf_op jit(solution)/shard_map/qd,kd->qk/dot_general | solution.py:120
  187.1 4.9 %fusion.121 = (f32[512]{0:T(512)S(1)}, f32[512,4352]{1,0:T(8,128)}) fusion(bf16[8704,512]{1,0:T(8,128)(2,1)S(1)} %bitcast.52, bf16[512,2,128]{2,0,1:T(8,128)(2,1)S(1)} %copy-done.8, s32[512]{0:T(512)S(1)} %convert_reduce_fusion.2, s32[4352]{0:T(1024)S(1)} %get-tuple-element.12, s32[512]{0:T(512)S(1)} %iota_add_fusion.2, s32[4352]{0:T(1024)S(1)} %iota_add_fusion), kind=kOutput, calls=%fused_computation.158 | convolution fusion | flops 583794176 | bytes 10205184 | tf_op jit(solution)/shard_map/qd,kd->qk/dot_general | solution.py:120
  192.0 4.9 %fusion.118 = (f32[512]{0:T(512)S(1)}, f32[512,4352]{1,0:T(8,128)}) fusion(bf16[8704,512]{1,0:T(8,128)(2,1)S(1)} %bitcast.53, bf16[512,2,128]{2,0,1:T(8,128)(2,1)S(1)} %copy-done.8, s32[512]{0:T(512)S(1)} %convert_reduce_fusion.2, s32[4352]{0:T(1024)S(1)} %get-tuple-element.12, s32[512]{0:T(512)S(1)} %iota_add_fusion.2, s32[4352]{0:T(1024)S(1)} %iota_add_fusion), kind=kOutput, calls=%fused_computation.155 | convolution fusion | flops 583794176 | bytes 10205184 | tf_op jit(solution)/shard_map/qd,kd->qk/dot_general | solution.py:120
  196.8 11.7 %fusion.4 = (f32[512]{0:T(512)S(1)}, f32[512]{0:T(512)S(1)}, f32[512]{0:T(512)S(1)}, f32[512]{0:T(512)S(1)}) fusion(f32[512,4352]{1,0:T(8,128)S(1)} %get-tuple-element.36, f32[512]{0:T(512)S(1)} %get-tuple-element.35, s32[512]{0:T(512)S(1)} %convert_reduce_fusion.2, s32[4352]{0:T(1024)S(1)} %get-tuple-element.11, s32[512]{0:T(512)S(1)} %iota_add_fusion.2, ...), kind=kLoop, calls=%fused_computation.15 | loop fusion | flops 40105984 | bytes 35741696 | tf_op jit(solution)/shard_map/reduce_sum | solution.py:124
  208.6 7.0 %fusion.57 = f32[512,256]{0,1:T(8,128)} fusion(bf16[8704,512]{1,0:T(8,128)(2,1)S(1)} %bitcast.54, f32[512,4352]{1,0:T(8,128)} %get-tuple-element.40, f32[512]{0:T(512)S(1)} %get-tuple-element.39, f32[512]{0:T(512)S(1)} %get-tuple-element.15, s32[4352]{0:T(1024)S(1)} %get-tuple-element.12, s32[4352]{0:T(1024)S(1)} %iota_add_fusion, ...), kind=kOutput, calls=%fused_computation.48 | convolution fusion | flops 1154351104 | bytes 11714560 | tf_op jit(solution)/shard_map/dot_general | solution.py:125
  215.6 6.0 %fusion.42 = f32[512,256]{0,1:T(8,128)S(1)} fusion(bf16[8704,512]{1,0:T(8,128)(2,1)S(1)} %bitcast.55, f32[512,4352]{1,0:T(8,128)} %get-tuple-element.34, f32[512]{0:T(512)S(1)} %get-tuple-element.33, f32[512]{0:T(512)S(1)} %get-tuple-element.44, s32[4352]{0:T(1024)S(1)} %get-tuple-element.12, s32[4352]{0:T(1024)S(1)} %iota_add_fusion, ...), kind=kOutput, calls=%fused_computation.45 | convolution fusion | flops 1154351104 | bytes 11714560 | tf_op jit(solution)/shard_map/dot_general | solution.py:125
  221.6 3.6 %fusion.81 = f32[512,256]{0,1:T(8,128)} fusion(f32[512,256]{0,1:T(8,128)S(1)} %fusion.42, bf16[8704,512]{1,0:T(8,128)(2,1)S(1)} %bitcast.56, f32[512,4352]{1,0:T(8,128)S(1)} %get-tuple-element.38, f32[512]{0:T(512)S(1)} %get-tuple-element.37, f32[512]{0:T(512)S(1)} %get-tuple-element.43, f32[512]{0:T(512)S(1)} %get-tuple-element.45, ...), kind=kOutput, calls=%fused_computation.57 | convolution fusion | flops 1154613248 | bytes 12240896 | tf_op jit(solution)/shard_map/dot_general | solution.py:125
  225.2 4.8 %multiply_reduce_fusion = (f32[512]{0:T(512)S(1)}, f32[512,256]{0,1:T(8,128)S(1)}) fusion(f32[512,256]{0,1:T(8,128)} %fusion.81, f32[512]{0:T(512)S(1)} %get-tuple-element.13, f32[512,256]{0,1:T(8,128)} %fusion.57, f32[512]{0:T(512)S(1)} %get-tuple-element.14, bf16[8704,512]{1,0:T(8,128)(2,1)S(1)} %bitcast.57, f32[512,4352]{1,0:T(8,128)S(1)} %get-tuple-element.36, ...), kind=kOutput, calls=%fused_computation.60 | convolution fusion | flops 1155137024 | bytes 12767236 | tf_op jit(solution)/shard_map/dot_general | solution.py:125
  231.0 1.0 collective-permute-done.3
  232.0 1.7 convolution_convert_fusion
  234.5 66.1 %all-reduce.2.cloned.1.call-done = bf16[256,2048]{1,0:T(8,128)(2,1)} async-done(((bf16[256,2048]{1,0:T(8,128)(2,1)}), bf16[256,2048]{1,0:T(8,128)(2,1)}) %all-reduce.2.cloned.1.call-update) | async-done | bytes 1048592 | tf_op jit(solution)/shard_map/psum | solution.py:157
  300.6 2.6 fusion.27
  (69 shorter events, 12.7 us)
Async XLA Ops:
  7.2 224.8 %copy-start = (bf16[512,2048]{1,0:T(8,128)(2,1)S(1)}, bf16[512,2048]{1,0:T(8,128)(2,1)}, u32[]{:S(2)}) copy-start(bf16[512,2048]{1,0:T(8,128)(2,1)} %param.14) | copy-start | bytes 6291460
  7.2 161.6 %all-gather.2.cloned.1.call-start = ((), (), s32[]{:S(2)}) async-start(), calls=%async_computation | async-start | bytes 17825792 | tf_op jit(solution)/shard_map/all_gather | solution.py:87
  14.2 0.7 copy-start.6
  15.6 35.5 %copy-start.2 = (bf16[256,2048]{1,0:T(8,128)(2,1)S(1)}, bf16[256,2048]{1,0:T(8,128)(2,1)}, u32[]{:S(2)}) copy-start(bf16[256,2048]{1,0:T(8,128)(2,1)} %param.9) | copy-start | bytes 3145732
  16.3 37.9 %copy-start.4 = (bf16[256,2,2,128]{3,2,1,0:T(2,128)(2,1)}, bf16[256,2,2,128]{3,2,1,0:T(2,128)(2,1)S(1)}, u32[]{:S(2)}) copy-start(bf16[256,2,2,128]{3,2,1,0:T(2,128)(2,1)S(1)} %maximum_convert_fusion) | copy-start | bytes 786436
  21.2 37.9 %copy-start.9 = (f32[4,2,128]{2,1,0:T(2,128)S(1)}, f32[4,2,128]{2,1,0:T(2,128)}, u32[]{:S(2)}) copy-start(f32[4,2,128]{2,1,0:T(2,128)} %param.15) | copy-start | bytes 12292
  23.0 36.5 %copy-start.10 = (f32[2,256]{1,0:T(2,128)S(1)}, f32[2,256]{1,0:T(2,128)}, u32[]{:S(2)}) copy-start(f32[2,256]{1,0:T(2,128)} %param.16) | copy-start | bytes 6148
  26.9 6.7 %collective-permute-start.1 = (bf16[256,512]{1,0:T(8,128)(2,1)}, bf16[256,512]{1,0:T(8,128)(2,1)}, u32[]{:S(2)}, u32[]{:S(2)}) collective-permute-start(bf16[256,512]{1,0:T(8,128)(2,1)} %pad_maximum_fusion), channel_id=1, source_target_pairs={{0,4},{4,0},{1,5},{5,1},{2,6},{6,2},{3,7},{7,3},{8,12},{12,8},{9,1... | collective-permute-start | bytes 786440 | tf_op jit(solution)/shard_map/ppermute | solution.py:39
  35.3 13.9 %collective-permute-start.2 = (bf16[512,512]{1,0:T(8,128)(2,1)}, bf16[512,512]{1,0:T(8,128)(2,1)}, u32[]{:S(2)}, u32[]{:S(2)}) collective-permute-start(bf16[512,512]{1,0:T(8,128)(2,1)} %constant_dynamic-update-slice_fusion.2), channel_id=1, source_target_pairs={{0,32},{32,0},{1,33},{33,1},{2,34},{34,2},{3,35},{35,3},{4,36},{36... | collective-permute-start | bytes 1572872 | tf_op jit(solution)/shard_map/ppermute | solution.py:85
  51.0 249.6 %all-reduce.2.cloned.1.call-start = ((), (), s32[]{:S(2)}) async-start(), calls=%async_computation.1 | async-start | bytes 2097152 | tf_op jit(solution)/shard_map/psum | solution.py:157
  58.1 2.3 collective-permute-start
  60.4 119.2 %copy-start.7 = (bf16[512,2,128]{2,0,1:T(8,128)(2,1)}, bf16[512,2,128]{2,0,1:T(8,128)(2,1)S(1)}, u32[]{:S(2)}) copy-start(bf16[512,2,128]{2,0,1:T(8,128)(2,1)S(1)} %constant_dynamic-update-slice_fusion.3) | copy-start | bytes 786436
  179.6 4.0 %copy-start.1 = (bf16[17,512,512]{2,1,0:T(8,128)(2,1)S(1)}, bf16[17,512,512]{2,1,0:T(8,128)(2,1)}, u32[]{:S(2)}) copy-start(bf16[17,512,512]{2,1,0:T(8,128)(2,1)} %gather_fusion) | copy-start | bytes 26738692
  183.5 3.6 %copy-start.8 = (bf16[512,2,128]{2,0,1:T(8,128)(2,1)S(1)}, bf16[512,2,128]{2,0,1:T(8,128)(2,1)}, u32[]{:S(2)}) copy-start(bf16[512,2,128]{2,0,1:T(8,128)(2,1)} %copy-done.7) | copy-start | bytes 786436
  225.2 8.5 %copy-start.5 = (bf16[256,2,2,128]{3,2,1,0:T(2,128)(2,1)S(1)}, bf16[256,2,2,128]{3,2,1,0:T(2,128)(2,1)}, u32[]{:S(2)}) copy-start(bf16[256,2,2,128]{3,2,1,0:T(2,128)(2,1)} %copy-done.4) | copy-start | bytes 786436
  225.2 75.4 %copy-start.3 = (bf16[256,2048]{1,0:T(8,128)(2,1)S(1)}, bf16[256,2048]{1,0:T(8,128)(2,1)}, u32[]{:S(2)}) copy-start(bf16[256,2048]{1,0:T(8,128)(2,1)} %param.9) | copy-start | bytes 3145732
  230.2 1.8 collective-permute-start.3
Sparse Core Ops, SparseCore 0:
  51.1 117.6 all-gather.1
  233.8 66.7 all-reduce.1

commit v4 on v3

--- a/solution.py
+++ b/solution.py
@@ -95,24 +95,15 @@
         core == 0,
     )
 
-    reach = min(MAXLEN // span + 1, chips)
+    reach = min(MAXLEN // span, chips - 1)
     window = reach * span
     base = chip * span
-    first_chip = jnp.clip(chip + 1 - reach, 0, chips - reach)
+    first_chip = jnp.clip(chip - reach, 0, chips - reach)
     start = first_chip * span
-    c = first_chip + jnp.arange(reach, dtype=jnp.int32)
-    slot = ((c // (zs * xs)) * xs + c % xs) * zs + (c // xs) % zs
-    kv_window = jnp.take(gathered.reshape(chips, span, -1), slot, axis=0, mode="clip").reshape(window, -1)
     q_index = base + jnp.arange(span, dtype=jnp.int32)
     q_seg, unused = locate(q_index, lengths)
-    pieces = 2
-    piece = window // pieces
 
-    def part(p):
-        key_index = start + p * piece + jnp.arange(piece, dtype=jnp.int32)
-        k_seg, unused = locate(key_index, lengths)
-        allowed = (key_index[None, :] <= q_index[:, None]) & (k_seg[None, :] == q_seg[:, None])
-        kv_win = kv_window[p * piece : (p + 1) * piece]
+    def stats_of(kv_win, key_index, allowed):
         v_win = kv_win[:, 2 * QK :]
         stats = []
         for m in range(2):
@@ -126,7 +117,23 @@
             stats.append((top, mass, acc))
         return stats
 
-    all_stats = [part(p) for p in range(pieces)]
+    local_allowed = (q_index[None, :] <= q_index[:, None]) & (q_seg[None, :] == q_seg[:, None])
+    local_stats = stats_of(kv_pair, q_index, local_allowed)
+    local_stats, gathered = lax.optimization_barrier((local_stats, gathered))
+
+    c = first_chip + jnp.arange(reach, dtype=jnp.int32)
+    slot = ((c // (zs * xs)) * xs + c % xs) * zs + (c // xs) % zs
+    kv_window = jnp.take(gathered.reshape(chips, span, -1), slot, axis=0, mode="clip").reshape(window, -1)
+    pieces = 2
+    piece = window // pieces
+
+    def part(p):
+        key_index = start + p * piece + jnp.arange(piece, dtype=jnp.int32)
+        k_seg, unused = locate(key_index, lengths)
+        allowed = (key_index[None, :] < base) & (k_seg[None, :] == q_seg[:, None])
+        return stats_of(kv_window[p * piece : (p + 1) * piece], key_index, allowed)
+
+    all_stats = [local_stats] + [part(p) for p in range(pieces)]
 
     def attend(m):
         tops = [stats[m][0] for stats in all_stats]

time: 311 us -> 302 us (0.971)
  waiting for transfers between devices: 186 us -> 179 us
  matrix products: 49.6 us -> 45.6 us
    all_gather x1, waiting for transfers between devices: 108 us -> 101 us  [on_device(): gathered = lax.all_gather(kv_quad, ('y', 'x'), axis=0, tiled=True)]
    slice x0 -> x1, local copies, waits for them, and re-layouts: none -> 3.85 us  [part(): return stats_of(kv_window[p * piece:(p + 1) * piece], key_index, allowed)]
    dot_general x8 -> x12, matrix products: 38.6 us -> 35.3 us  [the longest x6 19.8 us: stats_of(): jnp.dot(weights.astype(jnp.bfloat16), v_win, preferred_element_type=jnp.f...]
    reduce_sum x1 -> x2, other arithmetic: 11.7 us -> 11.4 us  [stats_of(): mass = jnp.sum(weights, axis=-1, keepdims=True)]
  transfers between devices with their start and end apart: 6 -> 6, of which waited for: 4 -> 4; matrix products, arithmetic and copies ran while one was open for 5% -> 8% of each run, Pallas kernels for 0% -> 0%
where the time goes in v4:
time: 302 us; the launch traced here: 301 us
  waiting for transfers between devices  179 us (59%)
  matrix products  45.6 us (15%)
  local copies, waits for them, and re-layouts  32.2 us (11%)
  other arithmetic  24.7 us (8%)
  between operations  14.4 us (5%)
  starting transfers between devices  5.18 us (2%)
    all_gather x1, waiting for transfers between devices, on_device(): gathered = lax.all_gather(kv_quad, ('y', 'x'), axis=0, tiled=True)  101 us
    psum x1, waiting for transfers between devices, on_device(): lax.psum(jnp.dot(merged, w_out, preferred_element_type=jnp.float32).astyp...  66.2 us
    dot_general x6, matrix products, stats_of(): jnp.dot(weights.astype(jnp.bfloat16), v_win, preferred_element_type=jnp.f...  19.8 us
    dot_general x6, matrix products, stats_of(): jnp.einsum('qd,kd->qk', q_pair[:, m, :], k_m, preferred_element_type=jnp....  15.5 us
    reduce_sum x2, other arithmetic, stats_of(): mass = jnp.sum(weights, axis=-1, keepdims=True)  11.4 us
    ppermute x1, waiting for transfers between devices, on_device(): kv_z = lax.ppermute(kv_pair, 'z', [(0, 1), (1, 0)])  11 us
    gather x1, local copies, waits for them, and re-layouts, on_device(): jnp.take(gathered.reshape(chips, span, -1), slot, axis=0, mode='clip')  10.5 us
  transfers between devices with their start and end apart: 6, of which 4 were waited for; matrix products, arithmetic and copies ran while one was open for 8% of the time, Pallas kernels for 0%

profile of v4, /device:TPU:1, one launch (start us, length us, event | category | flops | bytes accessed | tf_op | source)
XLA Modules:
  0.0 301.0 jit_solution(16174776558901243831)
XLA Ops:
  9.1 1.5 fusion.16
  10.6 2.7 fusion.128
  17.2 2.7 convolution_convert_fusion.1
  21.4 2.4 constant_dynamic-slice_fusion.3
  23.8 1.6 pad_maximum_fusion
  25.4 3.2 %collective-permute-start.1 = (bf16[256,512]{1,0:T(8,128)(2,1)}, bf16[256,512]{1,0:T(8,128)(2,1)}, u32[]{:S(2)}, u32[]{:S(2)}) collective-permute-start(bf16[256,512]{1,0:T(8,128)(2,1)} %pad_maximum_fusion), channel_id=1, source_target_pairs={{0,4},{4,0},{1,5},{5,1},{2,6},{6,2},{3,7},{7,3},{8,12},{12,8},{9,1... | collective-permute-start | bytes 786440 | tf_op jit(solution)/shard_map/ppermute | solution.py:39
  32.1 1.7 constant_dynamic-update-slice_fusion.2
  34.8 1.9 constant_dynamic-update-slice_fusion.1
  36.7 11.0 %collective-permute-done.2 = bf16[512,512]{1,0:T(8,128)(2,1)} collective-permute-done((bf16[512,512]{1,0:T(8,128)(2,1)}, bf16[512,512]{1,0:T(8,128)(2,1)}, u32[]{:S(2)}, u32[]{:S(2)}) %collective-permute-start.2) | collective-permute-done | bytes 524320 | tf_op jit(solution)/shard_map/ppermute | solution.py:85
  47.6 1.9 constant_dynamic-update-slice_fusion
  49.6 3.2 %fusion.130 = f32[256,512]{1,0:T(8,128)} fusion(bf16[2048,512]{1,0:T(8,128)(2,1)} %param.11, bf16[256,2048]{1,0:T(8,128)(2,1)S(1)} %copy-done.1, f32[2048]{0:T(1024)} %param.10, f32[256]{0:T(256)S(1)} %add_rsqrt_fusion.1), kind=kOutput, calls=%fused_computation.173 | convolution fusion | flops 538968064 | bytes 3679232 | tf_op jit(solution)/shard_map/dot_general | solution.py:89
  52.8 1.4 reshape.326
  54.1 1.7 add_convert_fusion
  58.9 1.3 fusion.134
  60.2 1.3 fusion.133
  61.9 2.3 fusion.94
  64.3 2.4 fusion.96
  66.6 100.7 %all-gather.2.cloned.1.call-done = bf16[16384,512]{1,0:T(8,128)(2,1)} async-done(((bf16[1024,512]{1,0:T(8,128)(2,1)}), bf16[16384,512]{1,0:T(8,128)(2,1)}) %all-gather.2.cloned.1.call-update) | async-done | bytes 16777232 | tf_op jit(solution)/shard_map/all_gather | solution.py:87
  167.3 10.5 %gather_fusion = bf16[16,512,512]{2,1,0:T(8,128)(2,1)} fusion(bf16[32,512,512]{2,1,0:T(8,128)(2,1)} %bitcast.77, s32[1024]{0:T(1024)S(1)} %pad_clamp_fusion), kind=kCustom, calls=%fused_computation | custom fusion | bytes 16777280 | tf_op jit(solution)/shard_map/jit(_take)/gather | solution.py:126
  177.8 3.8 %fusion.132 = (bf16[8,512,512]{2,1,0:T(8,128)(2,1)S(1)}, bf16[8,512,512]{2,1,0:T(8,128)(2,1)S(1)}) fusion(bf16[16,512,512]{2,1,0:T(8,128)(2,1)} %gather_fusion), kind=kLoop, calls=%fused_computation.174 | loop fusion | bytes 16777216 | tf_op jit(solution)/shard_map/slice | solution.py:134
  181.7 2.4 fusion.137
  184.1 2.4 fusion.136
  186.5 4.6 %fusion.138 = (f32[512]{0:T(512)S(1)}, f32[512,4096]{1,0:T(8,128)}) fusion(bf16[4096,512]{1,0:T(8,128)(2,1)S(1)} %bitcast.82, bf16[512,2,128]{2,0,1:T(8,128)(2,1)S(1)} %constant_dynamic-update-slice_fusion.3, s32[512]{0:T(512)S(1)} %convert_reduce_fusion.2, s32[4096]{0:T(1024)S(1)} %get-tuple-element.28, pred[4096]{0:T(1024)(128)(4,1)S(1)} %get-tuple-element.67), kind=kOutput, calls=%fused_computation.180 | convolution fusion | flops 547356160 | bytes 9592832 | tf_op jit(solution)/shard_map/qd,kd->qk/dot_general | solution.py:111
  191.1 3.6 %fusion.135 = (f32[512]{0:T(512)S(1)}, f32[512,4096]{1,0:T(8,128)S(1)}) fusion(bf16[4096,512]{1,0:T(8,128)(2,1)} %bitcast.83, bf16[512,2,128]{2,0,1:T(8,128)(2,1)S(1)} %constant_dynamic-update-slice_fusion.3, s32[512]{0:T(512)S(1)} %convert_reduce_fusion.2, s32[4096]{0:T(1024)S(1)} %get-tuple-element.28, pred[4096]{0:T(1024)(128)(4,1)S(1)} %get-tuple-element.67), kind=kOutput, calls=%fused_computation.177 | convolution fusion | flops 547356160 | bytes 9592832 | tf_op jit(solution)/shard_map/qd,kd->qk/dot_general | solution.py:111
  194.6 11.0 %fusion.4 = (f32[512]{0:T(512)S(1)}, f32[512]{0:T(512)S(1)}, f32[512]{0:T(512)S(1)}, f32[512]{0:T(512)S(1)}) fusion(f32[512,4096]{1,0:T(8,128)S(1)} %get-tuple-element.60, f32[512]{0:T(512)S(1)} %get-tuple-element.59, s32[4096]{0:T(1024)S(1)} %get-tuple-element.27, s32[512]{0:T(512)S(1)} %convert_reduce_fusion.2, pred[4096]{0:T(1024)(128)(4,1)S(1)} %get-tuple-element.68, ...), kind=kLoop, calls=%fused_computation.15 | loop fusion | flops 33552384 | bytes 33613824 | tf_op jit(solution)/shard_map/reduce_sum | solution.py:115
  205.6 5.6 %fusion.61 = f32[512,256]{1,0:T(8,128)S(1)} fusion(bf16[4096,512]{1,0:T(8,128)(2,1)} %bitcast.84, f32[512,4096]{1,0:T(8,128)} %get-tuple-element.64, f32[512]{0:T(512)S(1)} %get-tuple-element.63, s32[4096]{0:T(1024)S(1)} %get-tuple-element.28, s32[512]{0:T(512)S(1)} %convert_reduce_fusion.2, pred[4096]{0:T(1024)(128)(4,1)S(1)} %get-tuple-element.67, ...), kind=kOutput, calls=%fused_computation.46 | convolution fusion | flops 1084358656 | bytes 11036672 | tf_op jit(solution)/shard_map/dot_general | solution.py:116
  211.3 3.9 %fusion.41 = f32[512,256]{1,0:T(8,128)S(1)} fusion(bf16[4096,512]{1,0:T(8,128)(2,1)} %bitcast.85, f32[512,4096]{1,0:T(8,128)S(1)} %get-tuple-element.58, f32[512]{0:T(512)S(1)} %get-tuple-element.57, s32[4096]{0:T(1024)S(1)} %get-tuple-element.28, s32[512]{0:T(512)S(1)} %convert_reduce_fusion.2, pred[4096]{0:T(1024)(128)(4,1)S(1)} %get-tuple-element.67, ...), kind=kOutput, calls=%fused_computation.42 | convolution fusion | flops 1084358656 | bytes 11036672 | tf_op jit(solution)/shard_map/dot_general | solution.py:116
  215.3 2.4 fusion.85
  217.7 3.2 %multiply_reduce_fusion = (f32[512]{0:T(512)S(1)}, f32[512,256]{1,0:T(8,128)S(1)}) fusion(f32[512,256]{1,0:T(8,128)S(1)} %fusion.85, f32[512]{0:T(512)S(1)} %bitcast.109, f32[512,256]{1,0:T(8,128)S(1)} %fusion.61, f32[512]{0:T(512)S(1)} %bitcast.111, bf16[4096,512]{1,0:T(8,128)(2,1)S(1)} %bitcast.81, f32[512,4096]{1,0:T(8,128)S(1)} %get-tuple-element.60, ...), kind=kOutput, calls=%fused_computation.67 | convolution fusion | flops 1085406720 | bytes 12615684 | tf_op jit(solution)/shard_map/dot_general | solution.py:116
  222.8 1.7 convolution_convert_fusion
  225.3 66.2 %all-reduce.2.cloned.1.call-done = bf16[256,2048]{1,0:T(8,128)(2,1)} async-done(((bf16[256,2048]{1,0:T(8,128)(2,1)}), bf16[256,2048]{1,0:T(8,128)(2,1)}) %all-reduce.2.cloned.1.call-update) | async-done | bytes 1048592 | tf_op jit(solution)/shard_map/psum | solution.py:164
  291.6 2.6 fusion.19
  (75 shorter events, 18.0 us)
Async XLA Ops:
  7.2 215.6 %copy-start = (bf16[512,2048]{1,0:T(8,128)(2,1)S(1)}, bf16[512,2048]{1,0:T(8,128)(2,1)}, u32[]{:S(2)}) copy-start(bf16[512,2048]{1,0:T(8,128)(2,1)} %param.14) | copy-start | bytes 6291460
  7.2 160.1 %all-gather.2.cloned.1.call-start = ((), (), s32[]{:S(2)}) async-start(), calls=%async_computation | async-start | bytes 17825792 | tf_op jit(solution)/shard_map/all_gather | solution.py:87
  14.2 5.7 %copy-start.4 = (f32[256,64]{1,0:T(8,128)}, f32[256,64]{1,0:T(8,128)S(1)}, u32[]{:S(2)}) copy-start(f32[256,64]{1,0:T(8,128)S(1)} %get-tuple-element.52) | copy-start | bytes 196612
  19.9 0.7 copy-start.5
  21.4 28.2 %copy-start.1 = (bf16[256,2048]{1,0:T(8,128)(2,1)S(1)}, bf16[256,2048]{1,0:T(8,128)(2,1)}, u32[]{:S(2)}) copy-start(bf16[256,2048]{1,0:T(8,128)(2,1)} %param.9) | copy-start | bytes 3145732
  25.4 6.7 %collective-permute-start.1 = (bf16[256,512]{1,0:T(8,128)(2,1)}, bf16[256,512]{1,0:T(8,128)(2,1)}, u32[]{:S(2)}, u32[]{:S(2)}) collective-permute-start(bf16[256,512]{1,0:T(8,128)(2,1)} %pad_maximum_fusion), channel_id=1, source_target_pairs={{0,4},{4,0},{1,5},{5,1},{2,6},{6,2},{3,7},{7,3},{8,12},{12,8},{9,1... | collective-permute-start | bytes 786440 | tf_op jit(solution)/shard_map/ppermute | solution.py:39
  33.7 13.9 %collective-permute-start.2 = (bf16[512,512]{1,0:T(8,128)(2,1)}, bf16[512,512]{1,0:T(8,128)(2,1)}, u32[]{:S(2)}, u32[]{:S(2)}) collective-permute-start(bf16[512,512]{1,0:T(8,128)(2,1)} %constant_dynamic-update-slice_fusion.2), channel_id=1, source_target_pairs={{0,32},{32,0},{1,33},{33,1},{2,34},{34,2},{3,35},{35,3},{4,36},{36... | collective-permute-start | bytes 1572872 | tf_op jit(solution)/shard_map/ppermute | solution.py:85
  49.5 8.2 %copy-start.6 = (f32[4,2,128]{2,1,0:T(2,128)S(1)}, f32[4,2,128]{2,1,0:T(2,128)}, u32[]{:S(2)}) copy-start(f32[4,2,128]{2,1,0:T(2,128)} %param.15) | copy-start | bytes 12292
  49.5 8.6 %copy-start.7 = (f32[2,256]{1,0:T(2,128)S(1)}, f32[2,256]{1,0:T(2,128)}, u32[]{:S(2)}) copy-start(f32[2,256]{1,0:T(2,128)} %param.16) | copy-start | bytes 6148
  49.5 242.0 %all-reduce.2.cloned.1.call-start = ((), (), s32[]{:S(2)}) async-start(), calls=%async_computation.1 | async-start | bytes 2097152 | tf_op jit(solution)/shard_map/psum | solution.py:164
  56.6 2.3 collective-permute-start
  181.7 4.8 %copy-start.3 = (bf16[8,512,512]{2,1,0:T(8,128)(2,1)}, bf16[8,512,512]{2,1,0:T(8,128)(2,1)S(1)}, u32[]{:S(2)}) copy-start(bf16[8,512,512]{2,1,0:T(8,128)(2,1)S(1)} %get-tuple-element.38) | copy-start | bytes 12582916
  211.3 4.0 %copy-start.9 = (f32[512,256]{1,0:T(8,128)S(1)}, f32[512,256]{1,0:T(8,128)}, u32[]{:S(2)}) copy-start(f32[512,256]{1,0:T(8,128)} %fusion.96) | copy-start | bytes 1572868
  215.3 2.4 copy-start.8
  220.8 70.7 %copy-start.2 = (bf16[256,2048]{1,0:T(8,128)(2,1)S(1)}, bf16[256,2048]{1,0:T(8,128)(2,1)}, u32[]{:S(2)}) copy-start(bf16[256,2048]{1,0:T(8,128)(2,1)} %param.9) | copy-start | bytes 3145732
  221.0 1.8 collective-permute-start.3
Sparse Core Ops, SparseCore 0:
  49.6 117.6 all-gather.1
  224.7 66.8 all-reduce.1

commit v5 on v4

--- a/solution.py
+++ b/solution.py
@@ -123,15 +123,17 @@
 
     c = first_chip + jnp.arange(reach, dtype=jnp.int32)
     slot = ((c // (zs * xs)) * xs + c % xs) * zs + (c // xs) % zs
-    kv_window = jnp.take(gathered.reshape(chips, span, -1), slot, axis=0, mode="clip").reshape(window, -1)
     pieces = 2
     piece = window // pieces
+    per_piece = reach // pieces
+    chip_blocks = gathered.reshape(chips, span, -1)
 
     def part(p):
         key_index = start + p * piece + jnp.arange(piece, dtype=jnp.int32)
         k_seg, unused = locate(key_index, lengths)
         allowed = (key_index[None, :] < base) & (k_seg[None, :] == q_seg[:, None])
-        return stats_of(kv_window[p * piece : (p + 1) * piece], key_index, allowed)
+        kv_piece = jnp.take(chip_blocks, slot[p * per_piece : (p + 1) * per_piece], axis=0, mode="clip")
+        return stats_of(kv_piece.reshape(piece, -1), key_index, allowed)
 
     all_stats = [local_stats] + [part(p) for p in range(pieces)]
 

time: 302 us -> 313 us (1.036)
  matrix products: 45.6 us -> 52.7 us
  local copies, waits for them, and re-layouts: 32.2 us -> 36.5 us
    dot_general x6, matrix products: 15.5 us -> 23.1 us  [stats_of(): jnp.einsum('qd,kd->qk', q_pair[:, m, :], k_m, preferred_element_type=jnp....]
    gather x1 -> x2, local copies, waits for them, and re-layouts: 10.5 us -> 17.2 us  [part(): jnp.take(chip_blocks, slot[p * per_piece:(p + 1) * per_piece], axis=0, mo...]
    slice x1, local copies, waits for them, and re-layouts: 3.85 us -> 0.07 us  [part(): slot[p * per_piece:(p + 1) * per_piece]]
  transfers between devices with their start and end apart: 6 -> 6, of which waited for: 4 -> 4; matrix products, arithmetic and copies ran while one was open for 8% -> 7% of each run, Pallas kernels for 0% -> 0%
where the time goes in v5:
time: 313 us; the launch traced here: 312 us
  waiting for transfers between devices  179 us (57%)
  matrix products  52.7 us (17%)
  local copies, waits for them, and re-layouts  36.5 us (12%)
  other arithmetic  24.7 us (8%)
  between operations  14.4 us (5%)
  starting transfers between devices  5.2 us (2%)
    all_gather x1, waiting for transfers between devices, on_device(): gathered = lax.all_gather(kv_quad, ('y', 'x'), axis=0, tiled=True)  101 us
    psum x1, waiting for transfers between devices, on_device(): lax.psum(jnp.dot(merged, w_out, preferred_element_type=jnp.float32).astyp...  66.2 us
    dot_general x6, matrix products, stats_of(): jnp.einsum('qd,kd->qk', q_pair[:, m, :], k_m, preferred_element_type=jnp....  23.1 us
    dot_general x6, matrix products, stats_of(): jnp.dot(weights.astype(jnp.bfloat16), v_win, preferred_element_type=jnp.f...  19.3 us
    gather x2, local copies, waits for them, and re-layouts, part(): jnp.take(chip_blocks, slot[p * per_piece:(p + 1) * per_piece], axis=0, mo...  17.2 us
    reduce_sum x2, other arithmetic, stats_of(): mass = jnp.sum(weights, axis=-1, keepdims=True)  11.4 us
    ppermute x1, waiting for transfers between devices, on_device(): kv_z = lax.ppermute(kv_pair, 'z', [(0, 1), (1, 0)])  11 us
  transfers between devices with their start and end apart: 6, of which 4 were waited for; matrix products, arithmetic and copies ran while one was open for 7% of the time, Pallas kernels for 0%

profile of v5, /device:TPU:1, one launch (start us, length us, event | category | flops | bytes accessed | tf_op | source)
XLA Modules:
  0.0 312.3 jit_solution(16470672640589711248)
XLA Ops:
  9.1 1.5 fusion.16
  10.6 2.7 fusion.127
  17.2 2.7 convolution_convert_fusion.1
  21.4 2.4 constant_dynamic-slice_fusion.3
  23.8 1.6 pad_maximum_fusion
  25.4 3.2 %collective-permute-start.1 = (bf16[256,512]{1,0:T(8,128)(2,1)}, bf16[256,512]{1,0:T(8,128)(2,1)}, u32[]{:S(2)}, u32[]{:S(2)}) collective-permute-start(bf16[256,512]{1,0:T(8,128)(2,1)} %pad_maximum_fusion), channel_id=1, source_target_pairs={{0,4},{4,0},{1,5},{5,1},{2,6},{6,2},{3,7},{7,3},{8,12},{12,8},{9,1... | collective-permute-start | bytes 786440 | tf_op jit(solution)/shard_map/ppermute | solution.py:39
  32.1 1.7 constant_dynamic-update-slice_fusion.2
  34.8 1.9 constant_dynamic-update-slice_fusion.1
  36.7 11.0 %collective-permute-done.2 = bf16[512,512]{1,0:T(8,128)(2,1)} collective-permute-done((bf16[512,512]{1,0:T(8,128)(2,1)}, bf16[512,512]{1,0:T(8,128)(2,1)}, u32[]{:S(2)}, u32[]{:S(2)}) %collective-permute-start.2) | collective-permute-done | bytes 524320 | tf_op jit(solution)/shard_map/ppermute | solution.py:85
  47.6 1.9 constant_dynamic-update-slice_fusion
  49.6 3.2 %fusion.129 = f32[256,512]{1,0:T(8,128)} fusion(bf16[2048,512]{1,0:T(8,128)(2,1)} %param.11, bf16[256,2048]{1,0:T(8,128)(2,1)S(1)} %copy-done.1, f32[2048]{0:T(1024)} %param.10, f32[256]{0:T(256)S(1)} %add_rsqrt_fusion.1), kind=kOutput, calls=%fused_computation.174 | convolution fusion | flops 538968064 | bytes 3679232 | tf_op jit(solution)/shard_map/dot_general | solution.py:89
  52.8 1.4 reshape.183
  54.1 1.7 add_convert_fusion
  59.0 1.3 fusion.133
  60.2 1.3 fusion.132
  62.0 2.3 fusion.94
  64.3 2.3 fusion.96
  66.6 100.7 %all-gather.2.cloned.1.call-done = bf16[16384,512]{1,0:T(8,128)(2,1)} async-done(((bf16[1024,512]{1,0:T(8,128)(2,1)}), bf16[16384,512]{1,0:T(8,128)(2,1)}) %all-gather.2.cloned.1.call-update) | async-done | bytes 16777232 | tf_op jit(solution)/shard_map/all_gather | solution.py:87
  167.3 8.6 %gather_fusion = bf16[8,512,512]{2,1,0:T(8,128)(2,1)} fusion(bf16[32,512,512]{2,1,0:T(8,128)(2,1)} %bitcast.79, s32[1024]{0:T(1024)S(1)} %get-tuple-element.70), kind=kCustom, calls=%fused_computation | custom fusion | bytes 8388640 | tf_op jit(solution)/shard_map/jit(_take)/gather | solution.py:135
  175.9 5.7 %fusion.135 = (f32[512]{0:T(512)S(1)}, f32[512,4096]{1,0:T(8,128)}) fusion(bf16[4096,512]{1,0:T(8,128)(2,1)} %bitcast.81, bf16[512,2,128]{2,0,1:T(8,128)(2,1)S(1)} %constant_dynamic-update-slice_fusion.3, s32[512]{0:T(512)S(1)} %convert_reduce_fusion.2, s32[4096]{0:T(1024)S(1)} %get-tuple-element.27, pred[4096]{0:T(1024)(128)(4,1)S(1)} %get-tuple-element.68), kind=kOutput, calls=%fused_computation.179 | convolution fusion | flops 547356160 | bytes 9592832 | tf_op jit(solution)/shard_map/qd,kd->qk/dot_general | solution.py:111
  181.7 5.7 %fusion.136 = (f32[512]{0:T(512)S(1)}, f32[512,4096]{1,0:T(8,128)}) fusion(bf16[4096,512]{1,0:T(8,128)(2,1)} %bitcast.82, bf16[512,2,128]{2,0,1:T(8,128)(2,1)S(1)} %constant_dynamic-update-slice_fusion.3, s32[512]{0:T(512)S(1)} %convert_reduce_fusion.2, s32[4096]{0:T(1024)S(1)} %get-tuple-element.27, pred[4096]{0:T(1024)(128)(4,1)S(1)} %get-tuple-element.68), kind=kOutput, calls=%fused_computation.180 | convolution fusion | flops 547356160 | bytes 9592832 | tf_op jit(solution)/shard_map/qd,kd->qk/dot_general | solution.py:111
  187.4 8.5 %gather_fusion.1 = bf16[8,512,512]{2,1,0:T(8,128)(2,1)} fusion(bf16[32,512,512]{2,1,0:T(8,128)(2,1)} %bitcast.80, s32[1024]{0:T(1024)S(1)} %get-tuple-element.69), kind=kCustom, calls=%fused_computation.1 | custom fusion | bytes 8388640 | tf_op jit(solution)/shard_map/jit(_take)/gather | solution.py:135
  195.9 6.7 %fusion.137 = (f32[512]{0:T(512)S(1)}, f32[512,4096]{1,0:T(8,128)}) fusion(bf16[4096,512]{1,0:T(8,128)(2,1)} %bitcast.85, bf16[512,2,128]{2,0,1:T(8,128)(2,1)S(1)} %constant_dynamic-update-slice_fusion.3, s32[512]{0:T(512)S(1)} %convert_reduce_fusion.2, s32[4096]{0:T(1024)S(1)} %get-tuple-element.28, pred[4096]{0:T(1024)(128)(4,1)S(1)} %get-tuple-element.67), kind=kOutput, calls=%fused_computation.181 | convolution fusion | flops 547356160 | bytes 9592832 | tf_op jit(solution)/shard_map/qd,kd->qk/dot_general | solution.py:111
  202.7 2.4 fusion.134
  206.5 10.9 %fusion.4 = (f32[512]{0:T(512)S(1)}, f32[512]{0:T(512)S(1)}, f32[512]{0:T(512)S(1)}, f32[512]{0:T(512)S(1)}) fusion(f32[512,4096]{1,0:T(8,128)S(1)} %bitcast.76, f32[512]{0:T(512)S(1)} %get-tuple-element.59, s32[4096]{0:T(1024)S(1)} %get-tuple-element.27, s32[512]{0:T(512)S(1)} %convert_reduce_fusion.2, pred[4096]{0:T(1024)(128)(4,1)S(1)} %get-tuple-element.68, ...), kind=kLoop, calls=%fused_computation.16 | loop fusion | flops 33552384 | bytes 33613824 | tf_op jit(solution)/shard_map/reduce_sum | solution.py:115
  217.4 5.1 %fusion.61 = f32[512,256]{1,0:T(8,128)S(1)} fusion(bf16[4096,512]{1,0:T(8,128)(2,1)S(1)} %bitcast.88, f32[512,4096]{1,0:T(8,128)} %get-tuple-element.64, f32[512]{0:T(512)S(1)} %get-tuple-element.63, s32[4096]{0:T(1024)S(1)} %get-tuple-element.28, s32[512]{0:T(512)S(1)} %convert_reduce_fusion.2, pred[4096]{0:T(1024)(128)(4,1)S(1)} %get-tuple-element.67, ...), kind=kOutput, calls=%fused_computation.47 | convolution fusion | flops 1084358656 | bytes 11036672 | tf_op jit(solution)/shard_map/dot_general | solution.py:116
  222.6 4.0 %fusion.41 = f32[512,256]{1,0:T(8,128)S(1)} fusion(bf16[4096,512]{1,0:T(8,128)(2,1)} %bitcast.86, f32[512,4096]{1,0:T(8,128)S(1)} %get-tuple-element.58, f32[512]{0:T(512)S(1)} %get-tuple-element.57, s32[4096]{0:T(1024)S(1)} %get-tuple-element.28, s32[512]{0:T(512)S(1)} %convert_reduce_fusion.2, pred[4096]{0:T(1024)(128)(4,1)S(1)} %get-tuple-element.67, ...), kind=kOutput, calls=%fused_computation.43 | convolution fusion | flops 1084358656 | bytes 11036672 | tf_op jit(solution)/shard_map/dot_general | solution.py:116
  226.7 2.4 fusion.85
  229.1 3.2 %multiply_reduce_fusion = (f32[512]{0:T(512)S(1)}, f32[512,256]{1,0:T(8,128)S(1)}) fusion(f32[512,256]{1,0:T(8,128)S(1)} %fusion.85, f32[512]{0:T(512)S(1)} %bitcast.112, f32[512,256]{1,0:T(8,128)S(1)} %fusion.61, f32[512]{0:T(512)S(1)} %bitcast.114, bf16[4096,512]{1,0:T(8,128)(2,1)S(1)} %bitcast.84, f32[512,4096]{1,0:T(8,128)S(1)} %bitcast.76, ...), kind=kOutput, calls=%fused_computation.68 | convolution fusion | flops 1085406720 | bytes 12615684 | tf_op jit(solution)/shard_map/dot_general | solution.py:116
  234.2 1.7 convolution_convert_fusion
  236.7 66.2 %all-reduce.2.cloned.1.call-done = bf16[256,2048]{1,0:T(8,128)(2,1)} async-done(((bf16[256,2048]{1,0:T(8,128)(2,1)}), bf16[256,2048]{1,0:T(8,128)(2,1)}) %all-reduce.2.cloned.1.call-update) | async-done | bytes 1048592 | tf_op jit(solution)/shard_map/psum | solution.py:166
  302.9 2.6 fusion.19
  (88 shorter events, 19.5 us)
Async XLA Ops:
  7.2 227.0 %copy-start = (bf16[512,2048]{1,0:T(8,128)(2,1)S(1)}, bf16[512,2048]{1,0:T(8,128)(2,1)}, u32[]{:S(2)}) copy-start(bf16[512,2048]{1,0:T(8,128)(2,1)} %param.14) | copy-start | bytes 6291460
  7.2 160.1 %all-gather.2.cloned.1.call-start = ((), (), s32[]{:S(2)}) async-start(), calls=%async_computation | async-start | bytes 17825792 | tf_op jit(solution)/shard_map/all_gather | solution.py:87
  14.2 5.7 %copy-start.5 = (f32[256,64]{1,0:T(8,128)}, f32[256,64]{1,0:T(8,128)S(1)}, u32[]{:S(2)}) copy-start(f32[256,64]{1,0:T(8,128)S(1)} %get-tuple-element.50) | copy-start | bytes 196612
  19.9 0.7 copy-start.6
  21.4 28.2 %copy-start.1 = (bf16[256,2048]{1,0:T(8,128)(2,1)S(1)}, bf16[256,2048]{1,0:T(8,128)(2,1)}, u32[]{:S(2)}) copy-start(bf16[256,2048]{1,0:T(8,128)(2,1)} %param.9) | copy-start | bytes 3145732
  25.4 6.7 %collective-permute-start.1 = (bf16[256,512]{1,0:T(8,128)(2,1)}, bf16[256,512]{1,0:T(8,128)(2,1)}, u32[]{:S(2)}, u32[]{:S(2)}) collective-permute-start(bf16[256,512]{1,0:T(8,128)(2,1)} %pad_maximum_fusion), channel_id=1, source_target_pairs={{0,4},{4,0},{1,5},{5,1},{2,6},{6,2},{3,7},{7,3},{8,12},{12,8},{9,1... | collective-permute-start | bytes 786440 | tf_op jit(solution)/shard_map/ppermute | solution.py:39
  33.7 13.9 %collective-permute-start.2 = (bf16[512,512]{1,0:T(8,128)(2,1)}, bf16[512,512]{1,0:T(8,128)(2,1)}, u32[]{:S(2)}, u32[]{:S(2)}) collective-permute-start(bf16[512,512]{1,0:T(8,128)(2,1)} %constant_dynamic-update-slice_fusion.2), channel_id=1, source_target_pairs={{0,32},{32,0},{1,33},{33,1},{2,34},{34,2},{3,35},{35,3},{4,36},{36... | collective-permute-start | bytes 1572872 | tf_op jit(solution)/shard_map/ppermute | solution.py:85
  49.5 8.3 %copy-start.7 = (f32[4,2,128]{2,1,0:T(2,128)S(1)}, f32[4,2,128]{2,1,0:T(2,128)}, u32[]{:S(2)}) copy-start(f32[4,2,128]{2,1,0:T(2,128)} %param.15) | copy-start | bytes 12292
  49.5 8.6 %copy-start.8 = (f32[2,256]{1,0:T(2,128)S(1)}, f32[2,256]{1,0:T(2,128)}, u32[]{:S(2)}) copy-start(f32[2,256]{1,0:T(2,128)} %param.16) | copy-start | bytes 6148
  49.5 253.4 %all-reduce.2.cloned.1.call-start = ((), (), s32[]{:S(2)}) async-start(), calls=%async_computation.1 | async-start | bytes 2097152 | tf_op jit(solution)/shard_map/psum | solution.py:166
  56.6 2.3 collective-permute-start
  195.9 6.8 %copy-start.4 = (bf16[8,512,512]{2,1,0:T(8,128)(2,1)S(1)}, bf16[8,512,512]{2,1,0:T(8,128)(2,1)}, u32[]{:S(2)}) copy-start(bf16[8,512,512]{2,1,0:T(8,128)(2,1)} %gather_fusion.1) | copy-start | bytes 12582916
  195.9 9.1 %slice-start = ((s8[8388608]{0:T(1024)(128)(4,1)}), s8[4194304]{0:T(1024)(128)(4,1)S(1)}, s32[]{:S(2)}) async-start(s8[8388608]{0:T(1024)(128)(4,1)} %bitcast.75), calls=%async_computation.2 | async-start | bytes 8388608
  195.9 9.2 %slice-start.2 = ((s8[8388608]{0:T(1024)(128)(4,1)}), s8[4194304]{0:T(1024)(128)(4,1)S(1)}, s32[]{:S(2)}) async-start(s8[8388608]{0:T(1024)(128)(4,1)} %bitcast.77), calls=%async_computation.4 | async-start | bytes 8388608
  202.6 2.6 slice-start.1
  202.6 3.8 %slice-start.3 = ((s8[8388608]{0:T(1024)(128)(4,1)}), s8[4194304]{0:T(1024)(128)(4,1)S(1)}, s32[]{:S(2)}) async-start(s8[8388608]{0:T(1024)(128)(4,1)} %bitcast.77), calls=%async_computation.5 | async-start | bytes 8388608
  222.6 4.1 %copy-start.3 = (bf16[8,512,512]{2,1,0:T(8,128)(2,1)S(1)}, bf16[8,512,512]{2,1,0:T(8,128)(2,1)}, u32[]{:S(2)}) copy-start(bf16[8,512,512]{2,1,0:T(8,128)(2,1)} %gather_fusion) | copy-start | bytes 12582916
  222.6 4.1 %copy-start.10 = (f32[512,256]{1,0:T(8,128)S(1)}, f32[512,256]{1,0:T(8,128)}, u32[]{:S(2)}) copy-start(f32[512,256]{1,0:T(8,128)} %fusion.96) | copy-start | bytes 1572868
  226.7 2.4 copy-start.9
  232.2 70.7 %copy-start.2 = (bf16[256,2048]{1,0:T(8,128)(2,1)S(1)}, bf16[256,2048]{1,0:T(8,128)(2,1)}, u32[]{:S(2)}) copy-start(bf16[256,2048]{1,0:T(8,128)(2,1)} %param.9) | copy-start | bytes 3145732
  232.4 1.8 collective-permute-start.3
Sparse Core Ops, SparseCore 0:
  49.6 117.6 all-gather.1
  236.1 66.8 all-reduce.1

commit v6 on v4

--- a/solution.py
+++ b/solution.py
@@ -80,10 +80,16 @@
         return lax.dynamic_update_slice_in_dim(both, theirs, jnp.where(first_is_mine, rows_each, 0), axis=0)
 
     span = 2 * rows
-    kv_pair = in_order(head_kv(core), swap_cores(head_kv(1 - core)), core == 0)
     z = lax.axis_index("z")
-    kv_z = lax.ppermute(kv_pair, "z", [(0, 1), (1, 0)])
-    kv_quad = in_order(kv_pair, kv_z, z == 0)
+    kv_both = jnp.stack([head_kv(0), head_kv(1)], axis=1)
+    kv_chips = in_order(kv_both, lax.ppermute(kv_both, "z", [(0, 1), (1, 0)]), z == 0)
+    mine = lax.dynamic_index_in_dim(kv_chips, core, axis=1, keepdims=False).reshape(2, rows, -1)
+    theirs = swap_cores(lax.dynamic_index_in_dim(kv_chips, 1 - core, axis=1, keepdims=False)).reshape(2, rows, -1)
+    quad = jnp.zeros((2, span, mine.shape[-1]), mine.dtype)
+    quad = lax.dynamic_update_slice_in_dim(quad, mine, core * rows, axis=1)
+    quad = lax.dynamic_update_slice_in_dim(quad, theirs, (1 - core) * rows, axis=1)
+    kv_quad = quad.reshape(2 * span, -1)
+    kv_pair = lax.dynamic_index_in_dim(quad, z, axis=0, keepdims=False)
     gathered = lax.all_gather(kv_quad, ("y", "x"), axis=0, tiled=True)
     query = rotate(
         jnp.dot(normed, w_query, preferred_element_type=jnp.float32).reshape(rows, heads, 2, QK),

time: 302 us -> 298 us (0.987)
  waiting for transfers between devices: 179 us -> 174 us
  other arithmetic: 24.7 us -> 28.4 us
    all_gather x1, waiting for transfers between devices: 101 us -> 94.8 us  [on_device(): gathered = lax.all_gather(kv_quad, ('y', 'x'), axis=0, tiled=True)]
  transfers between devices with their start and end apart: 6 -> 6, of which waited for: 4 -> 5; matrix products, arithmetic and copies ran while one was open for 8% -> 8% of each run, Pallas kernels for 0% -> 0%
where the time goes in v6:
time: 298 us; the launch traced here: 297 us
  waiting for transfers between devices  174 us (58%)
  matrix products  43.2 us (14%)
  local copies, waits for them, and re-layouts  31.2 us (10%)
  other arithmetic  28.4 us (10%)
  between operations  14.5 us (5%)
  starting transfers between devices  6.02 us (2%)
    all_gather x1, waiting for transfers between devices, on_device(): gathered = lax.all_gather(kv_quad, ('y', 'x'), axis=0, tiled=True)  94.8 us
    psum x1, waiting for transfers between devices, on_device(): lax.psum(jnp.dot(merged, w_out, preferred_element_type=jnp.float32).astyp...  66.1 us
    dot_general x6, matrix products, stats_of(): jnp.dot(weights.astype(jnp.bfloat16), v_win, preferred_element_type=jnp.f...  17 us
    dot_general x6, matrix products, stats_of(): jnp.einsum('qd,kd->qk', q_pair[:, m, :], k_m, preferred_element_type=jnp....  15.6 us
    reduce_sum x2, other arithmetic, stats_of(): mass = jnp.sum(weights, axis=-1, keepdims=True)  11.4 us
    ppermute x1, waiting for transfers between devices, on_device(): lax.ppermute(kv_both, 'z', [(0, 1), (1, 0)])  10.9 us
    gather x1, local copies, waits for them, and re-layouts, on_device(): jnp.take(gathered.reshape(chips, span, -1), slot, axis=0, mode='clip')  10.7 us
  transfers between devices with their start and end apart: 6, of which 5 were waited for; matrix products, arithmetic and copies ran while one was open for 8% of the time, Pallas kernels for 0%

profile of v6, /device:TPU:1, one launch (start us, length us, event | category | flops | bytes accessed | tf_op | source)
XLA Modules:
  0.0 296.9 jit_solution(10148170230024189681)
XLA Ops:
  9.1 1.5 fusion.16
  10.6 2.7 fusion.128
  16.6 2.7 convolution_convert_fusion.1
  22.5 2.5 collective-permute-start.1
  24.9 10.9 %collective-permute-done.1 = bf16[256,2,512]{2,0,1:T(8,128)(2,1)} collective-permute-done((bf16[256,2,512]{2,0,1:T(8,128)(2,1)}, bf16[256,2,512]{2,0,1:T(8,128)(2,1)}, u32[]{:S(2)}, u32[]{:S(2)}) %collective-permute-start.1) | collective-permute-done | bytes 524320 | tf_op jit(solution)/shard_map/ppermute | solution.py:85
  38.0 2.3 collective-permute-start.2
  40.3 1.1 constant_dynamic-update-slice_fusion.1
  42.1 1.1 constant_dynamic-update-slice_fusion
  44.3 3.6 %fusion.130 = f32[256,512]{1,0:T(8,128)} fusion(bf16[2048,512]{1,0:T(8,128)(2,1)} %param.11, bf16[256,2048]{1,0:T(8,128)(2,1)} %param.9, f32[2048]{0:T(1024)S(1)} %copy-done.16, f32[256]{0:T(256)S(1)} %add_rsqrt_fusion.1), kind=kOutput, calls=%fused_computation.174 | convolution fusion | flops 538968064 | bytes 3679232 | tf_op jit(solution)/shard_map/dot_general | solution.py:95
  47.8 2.2 reshape.336
  50.0 2.0 add_convert_fusion
  56.3 1.3 convert_reduce_fusion.2
  59.6 1.2 dynamic_slice.55
  61.7 1.6 constant_dynamic-update-slice_fusion.4
  63.3 1.3 fusion.136
  64.6 1.3 fusion.135
  66.9 1.4 fusion.96
  68.3 94.8 %all-gather.2.cloned.1.call-done = bf16[16384,512]{1,0:T(8,128)(2,1)} async-done(((bf16[1024,512]{1,0:T(8,128)(2,1)}), bf16[16384,512]{1,0:T(8,128)(2,1)}) %all-gather.2.cloned.1.call-update) | async-done | bytes 16777232 | tf_op jit(solution)/shard_map/all_gather | solution.py:93
  163.1 10.7 %gather_fusion = bf16[16,512,512]{2,1,0:T(8,128)(2,1)} fusion(bf16[32,512,512]{2,1,0:T(8,128)(2,1)} %bitcast.87, s32[1024]{0:T(1024)} %pad_clamp_fusion), kind=kCustom, calls=%fused_computation | custom fusion | bytes 16777280 | tf_op jit(solution)/shard_map/jit(_take)/gather | solution.py:132
  173.8 3.9 %fusion.132 = (bf16[8,512,512]{2,1,0:T(8,128)(2,1)S(1)}, bf16[8,512,512]{2,1,0:T(8,128)(2,1)S(1)}) fusion(bf16[16,512,512]{2,1,0:T(8,128)(2,1)} %gather_fusion), kind=kLoop, calls=%fused_computation.175 | loop fusion | bytes 16777216 | tf_op jit(solution)/shard_map/slice | solution.py:140
  177.7 2.4 fusion.139
  180.1 2.4 fusion.138
  182.5 4.6 %fusion.140 = (f32[512]{0:T(512)S(1)}, f32[512,4096]{1,0:T(8,128)}) fusion(bf16[4096,512]{1,0:T(8,128)(2,1)S(1)} %bitcast.92, bf16[512,2,128]{2,0,1:T(8,128)(2,1)S(1)} %copy-done.8, s32[512]{0:T(512)S(1)} %copy-done.9, s32[4096]{0:T(1024)S(1)} %get-tuple-element.28, pred[4096]{0:T(1024)(128)(4,1)S(1)} %copy-done.13), kind=kOutput, calls=%fused_computation.183 | convolution fusion | flops 547356160 | bytes 9592832 | tf_op jit(solution)/shard_map/qd,kd->qk/dot_general | solution.py:117
  187.1 3.6 %fusion.137 = (f32[512]{0:T(512)S(1)}, f32[512,4096]{1,0:T(8,128)S(1)}) fusion(bf16[4096,512]{1,0:T(8,128)(2,1)} %bitcast.93, bf16[512,2,128]{2,0,1:T(8,128)(2,1)S(1)} %copy-done.8, s32[512]{0:T(512)S(1)} %copy-done.9, s32[4096]{0:T(1024)S(1)} %get-tuple-element.28, pred[4096]{0:T(1024)(128)(4,1)S(1)} %copy-done.13), kind=kOutput, calls=%fused_computation.180 | convolution fusion | flops 547356160 | bytes 9592832 | tf_op jit(solution)/shard_map/qd,kd->qk/dot_general | solution.py:117
  190.7 11.0 %fusion.4 = (f32[512]{0:T(512)S(1)}, f32[512]{0:T(512)S(1)}, f32[512]{0:T(512)S(1)}, f32[512]{0:T(512)S(1)}) fusion(f32[512,4096]{1,0:T(8,128)S(1)} %get-tuple-element.64, f32[512]{0:T(512)S(1)} %get-tuple-element.63, s32[4096]{0:T(1024)S(1)} %get-tuple-element.27, s32[512]{0:T(512)S(1)} %copy-done.9, pred[4096]{0:T(1024)(128)(4,1)S(1)} %copy-done.12, ...), kind=kLoop, calls=%fused_computation.15 | loop fusion | flops 33552384 | bytes 33613824 | tf_op jit(solution)/shard_map/reduce_sum | solution.py:121
  201.7 5.6 %fusion.61 = f32[512,256]{1,0:T(8,128)S(1)} fusion(bf16[4096,512]{1,0:T(8,128)(2,1)} %bitcast.94, f32[512,4096]{1,0:T(8,128)} %get-tuple-element.68, f32[512]{0:T(512)S(1)} %get-tuple-element.67, s32[4096]{0:T(1024)S(1)} %get-tuple-element.28, s32[512]{0:T(512)S(1)} %copy-done.9, pred[4096]{0:T(1024)(128)(4,1)S(1)} %copy-done.13, f32[512]{0:T(512)S(1)} %bitcast.124), kind=kOutput, calls=%fused_computation.46 | convolution fusion | flops 1084358656 | bytes 11036672 | tf_op jit(solution)/shard_map/dot_general | solution.py:122
  207.4 3.9 %fusion.41 = f32[512,256]{1,0:T(8,128)S(1)} fusion(bf16[4096,512]{1,0:T(8,128)(2,1)} %bitcast.95, f32[512,4096]{1,0:T(8,128)S(1)} %get-tuple-element.62, f32[512]{0:T(512)S(1)} %get-tuple-element.61, s32[4096]{0:T(1024)S(1)} %get-tuple-element.28, s32[512]{0:T(512)S(1)} %copy-done.9, pred[4096]{0:T(1024)(128)(4,1)S(1)} %copy-done.13, f32[512]{0:T(512)S(1)} %bitcast.123), kind=kOutput, calls=%fused_computation.42 | convolution fusion | flops 1084358656 | bytes 11036672 | tf_op jit(solution)/shard_map/dot_general | solution.py:122
  211.3 2.4 fusion.85
  213.7 3.1 %multiply_reduce_fusion = (f32[512]{0:T(512)S(1)}, f32[512,256]{1,0:T(8,128)S(1)}) fusion(f32[512,256]{1,0:T(8,128)S(1)} %fusion.85, f32[512]{0:T(512)S(1)} %bitcast.117, f32[512,256]{1,0:T(8,128)S(1)} %fusion.61, f32[512]{0:T(512)S(1)} %bitcast.119, bf16[4096,512]{1,0:T(8,128)(2,1)S(1)} %bitcast.91, f32[512,4096]{1,0:T(8,128)S(1)} %get-tuple-element.64, ...), kind=kOutput, calls=%fused_computation.68 | convolution fusion | flops 1085406720 | bytes 12615684 | tf_op jit(solution)/shard_map/dot_general | solution.py:122
  218.8 1.7 convolution_convert_fusion
  221.3 66.1 %all-reduce.2.cloned.1.call-done = bf16[256,2048]{1,0:T(8,128)(2,1)} async-done(((bf16[256,2048]{1,0:T(8,128)(2,1)}), bf16[256,2048]{1,0:T(8,128)(2,1)}) %all-reduce.2.cloned.1.call-update) | async-done | bytes 1048592 | tf_op jit(solution)/shard_map/psum | solution.py:170
  287.4 2.6 fusion.19
  (93 shorter events, 23.2 us)
Async XLA Ops:
  7.2 211.7 %copy-start = (bf16[512,2048]{1,0:T(8,128)(2,1)S(1)}, bf16[512,2048]{1,0:T(8,128)(2,1)}, u32[]{:S(2)}) copy-start(bf16[512,2048]{1,0:T(8,128)(2,1)} %param.14) | copy-start | bytes 6291460
  7.2 156.0 %all-gather.2.cloned.1.call-start = ((), (), s32[]{:S(2)}) async-start(), calls=%async_computation | async-start | bytes 17825792 | tf_op jit(solution)/shard_map/all_gather | solution.py:93
  8.2 2.4 copy-start.14
  10.6 6.0 %copy-start.16 = (f32[2048]{0:T(1024)S(1)}, f32[2048]{0:T(1024)}, u32[]{:S(2)}) copy-start(f32[2048]{0:T(1024)} %param.10) | copy-start | bytes 24580
  14.2 5.9 %copy-start.5 = (f32[256,64]{1,0:T(8,128)}, f32[256,64]{1,0:T(8,128)S(1)}, u32[]{:S(2)}) copy-start(f32[256,64]{1,0:T(8,128)S(1)} %get-tuple-element.56) | copy-start | bytes 196612
  19.3 0.7 copy-start.6
  22.5 13.4 %collective-permute-start.1 = (bf16[256,2,512]{2,0,1:T(8,128)(2,1)}, bf16[256,2,512]{2,0,1:T(8,128)(2,1)}, u32[]{:S(2)}, u32[]{:S(2)}) collective-permute-start(bf16[256,2,512]{2,0,1:T(8,128)(2,1)} %get-tuple-element.47), channel_id=1, source_target_pairs={{0,32},{32,0},{1,33},{33,1},{2,34},{34,2},{3,35},{35,3},{4,36},{36... | collective-permute-start | bytes 1572872 | tf_op jit(solution)/shard_map/ppermute | solution.py:85
  38.0 4.2 %collective-permute-start.2 = (bf16[512,512]{1,0:T(8,128)(2,1)}, bf16[512,512]{1,0:T(8,128)(2,1)}, u32[]{:S(2)}, u32[]{:S(2)}) collective-permute-start(bf16[512,512]{1,0:T(8,128)(2,1)} %get-tuple-element.39), channel_id=1, source_target_pairs={{0,4},{4,0},{1,5},{5,1},{2,6},{6,2},{3,7},{7,3},{8,12},{12,8},{9,1... | collective-permute-start | bytes 1572872 | tf_op jit(solution)/shard_map/ppermute | solution.py:39
  43.2 1.0 copy-start.1
  44.2 11.4 %copy-start.15 = (f32[4,2,128]{2,1,0:T(2,128)S(1)}, f32[4,2,128]{2,1,0:T(2,128)}, u32[]{:S(2)}) copy-start(f32[4,2,128]{2,1,0:T(2,128)} %param.15) | copy-start | bytes 12292
  44.2 19.1 %copy-start.2 = (bf16[2,512,512]{2,1,0:T(8,128)(2,1)S(1)}, bf16[2,512,512]{2,1,0:T(8,128)(2,1)}, u32[]{:S(2)}) copy-start(bf16[2,512,512]{2,1,0:T(8,128)(2,1)} %copy-done.1) | copy-start | bytes 3145732
  44.2 243.2 %all-reduce.2.cloned.1.call-start = ((), (), s32[]{:S(2)}) async-start(), calls=%async_computation.1 | async-start | bytes 2097152 | tf_op jit(solution)/shard_map/psum | solution.py:170
  53.4 8.3 %collective-permute-start = (bf16[256,2,128]{2,0,1:T(8,128)(2,1)}, bf16[256,2,128]{2,0,1:T(8,128)(2,1)}, u32[]{:S(2)}, u32[]{:S(2)}) collective-permute-start(bf16[256,2,128]{2,0,1:T(8,128)(2,1)} %bitcast.85), channel_id=1, source_target_pairs={{0,4},{4,0},{1,5},{5,1},{2,6},{6,2},{3,7},{7,3},{8,12},{12,8},{9,1... | collective-permute-start | bytes 393224 | tf_op jit(solution)/shard_map/ppermute | solution.py:39
  53.8 4.3 %copy-start.10 = (s32[512]{0:T(512)}, s32[512]{0:T(512)S(1)}, u32[]{:S(2)}) copy-start(s32[512]{0:T(512)S(1)} %iota_add_fusion.2) | copy-start | bytes 6148
  58.2 0.7 copy-start.7
  58.9 7.0 %copy-start.9 = (s32[512]{0:T(512)S(1)}, s32[512]{0:T(512)}, u32[]{:S(2)}) copy-start(s32[512]{0:T(512)} %convert_reduce_fusion.2) | copy-start | bytes 6148
  58.9 7.0 %copy-start.11 = (s32[512]{0:T(512)S(1)}, s32[512]{0:T(512)}, u32[]{:S(2)}) copy-start(s32[512]{0:T(512)} %copy-done.10) | copy-start | bytes 6148
  173.8 3.9 %copy-start.8 = (bf16[512,2,128]{2,0,1:T(8,128)(2,1)S(1)}, bf16[512,2,128]{2,0,1:T(8,128)(2,1)}, u32[]{:S(2)}) copy-start(bf16[512,2,128]{2,0,1:T(8,128)(2,1)} %constant_dynamic-update-slice_fusion.4) | copy-start | bytes 786436
  173.8 3.9 %copy-start.12 = (pred[4096]{0:T(1024)(128)(4,1)S(1)}, pred[4096]{0:T(1024)(128)(4,1)}, u32[]{:S(2)}) copy-start(pred[4096]{0:T(1024)(128)(4,1)} %broadcast_compare_fusion.1) | copy-start | bytes 12292
  177.7 4.8 %copy-start.4 = (bf16[8,512,512]{2,1,0:T(8,128)(2,1)}, bf16[8,512,512]{2,1,0:T(8,128)(2,1)S(1)}, u32[]{:S(2)}) copy-start(bf16[8,512,512]{2,1,0:T(8,128)(2,1)S(1)} %get-tuple-element.38) | copy-start | bytes 12582916
  180.1 2.4 copy-start.13
  207.4 4.0 %copy-start.17 = (f32[512,256]{1,0:T(8,128)S(1)}, f32[512,256]{1,0:T(8,128)}, u32[]{:S(2)}) copy-start(f32[512,256]{1,0:T(8,128)} %fusion.96) | copy-start | bytes 1572868
  216.8 70.6 %copy-start.3 = (bf16[256,2048]{1,0:T(8,128)(2,1)S(1)}, bf16[256,2048]{1,0:T(8,128)(2,1)}, u32[]{:S(2)}) copy-start(bf16[256,2048]{1,0:T(8,128)(2,1)} %param.9) | copy-start | bytes 3145732
  217.0 1.8 collective-permute-start.3
Sparse Core Ops, SparseCore 0:
  44.3 118.7 all-gather.1
  220.7 66.7 all-reduce.1

commit v7 on v6

--- a/solution.py
+++ b/solution.py
@@ -82,7 +82,8 @@
     span = 2 * rows
     z = lax.axis_index("z")
     kv_both = jnp.stack([head_kv(0), head_kv(1)], axis=1)
-    kv_chips = in_order(kv_both, lax.ppermute(kv_both, "z", [(0, 1), (1, 0)]), z == 0)
+    halves = [lax.ppermute(kv_both[..., i * 2 * QK : (i + 1) * 2 * QK], "z", [(0, 1), (1, 0)]) for i in range(2)]
+    kv_chips = in_order(kv_both, jnp.concatenate(halves, axis=-1), z == 0)
     mine = lax.dynamic_index_in_dim(kv_chips, core, axis=1, keepdims=False).reshape(2, rows, -1)
     theirs = swap_cores(lax.dynamic_index_in_dim(kv_chips, 1 - core, axis=1, keepdims=False)).reshape(2, rows, -1)
     quad = jnp.zeros((2, span, mine.shape[-1]), mine.dtype)

time: 298 us -> 297 us (level)
    ppermute x1 -> x2, waiting for transfers between devices: 10.9 us -> 10.6 us  [on_device(): lax.ppermute(kv_both[..., i * 2 * QK:(i + 1) * 2 * QK], 'z', [(0, 1), (1,...]
  transfers between devices with their start and end apart: 6 -> 7, of which waited for: 5 -> 6; matrix products, arithmetic and copies ran while one was open for 8% -> 8% of each run, Pallas kernels for 0% -> 0%
where the time goes in v7:
time: 297 us
  waiting for transfers between devices  173 us (58%)
  matrix products  43.2 us (15%)
  local copies, waits for them, and re-layouts  30.1 us (10%)
  other arithmetic  29.3 us (10%)
  between operations  14.5 us (5%)
  starting transfers between devices  6.13 us (2%)
    all_gather x1, waiting for transfers between devices, on_device(): gathered = lax.all_gather(kv_quad, ('y', 'x'), axis=0, tiled=True)  94.9 us
    psum x1, waiting for transfers between devices, on_device(): lax.psum(jnp.dot(merged, w_out, preferred_element_type=jnp.float32).astyp...  66.2 us
    dot_general x6, matrix products, stats_of(): jnp.dot(weights.astype(jnp.bfloat16), v_win, preferred_element_type=jnp.f...  17 us
    dot_general x6, matrix products, stats_of(): jnp.einsum('qd,kd->qk', q_pair[:, m, :], k_m, preferred_element_type=jnp....  15.6 us
    reduce_sum x2, other arithmetic, stats_of(): mass = jnp.sum(weights, axis=-1, keepdims=True)  11.4 us
    gather x1, local copies, waits for them, and re-layouts, on_device(): jnp.take(gathered.reshape(chips, span, -1), slot, axis=0, mode='clip')  10.7 us
    ppermute x2, waiting for transfers between devices, on_device(): lax.ppermute(kv_both[..., i * 2 * QK:(i + 1) * 2 * QK], 'z', [(0, 1), (1,...  10.6 us
  transfers between devices with their start and end apart: 7, of which 6 were waited for; matrix products, arithmetic and copies ran while one was open for 8% of the time, Pallas kernels for 0%

profile of v7, /device:TPU:1, one launch (start us, length us, event | category | flops | bytes accessed | tf_op | source)
XLA Modules:
  0.0 296.7 jit_solution(17206890886922927815)
XLA Ops:
  9.1 1.5 fusion.16
  10.6 2.7 fusion.131
  16.6 2.7 convolution_convert_fusion.1
  22.2 2.5 collective-permute-start.1
  24.8 5.1 %collective-permute-done.1 = bf16[256,2,256]{2,0,1:T(8,128)(2,1)S(1)} collective-permute-done((bf16[256,2,256]{2,0,1:T(8,128)(2,1)}, bf16[256,2,256]{2,0,1:T(8,128)(2,1)S(1)}, u32[]{:S(2)}, u32[]{:S(2)}) %collective-permute-start.1) | collective-permute-done | bytes 262176 | tf_op jit(solution)/shard_map/ppermute | solution.py:85
  30.0 5.5 %collective-permute-done.2 = bf16[256,2,256]{2,0,1:T(8,128)(2,1)} collective-permute-done((bf16[256,2,256]{2,0,1:T(8,128)(2,1)S(1)}, bf16[256,2,256]{2,0,1:T(8,128)(2,1)}, u32[]{:S(2)}, u32[]{:S(2)}) %collective-permute-start.2) | collective-permute-done | bytes 262176 | tf_op jit(solution)/shard_map/ppermute | solution.py:85
  37.5 2.4 collective-permute-start.3
  40.0 1.1 constant_dynamic-update-slice_fusion.1
  43.9 3.6 %fusion.133 = f32[256,512]{1,0:T(8,128)} fusion(bf16[2048,512]{1,0:T(8,128)(2,1)} %param.11, bf16[256,2048]{1,0:T(8,128)(2,1)} %param.9, f32[2048]{0:T(1024)S(1)} %copy-done.16, f32[256]{0:T(256)S(1)} %add_rsqrt_fusion.1), kind=kOutput, calls=%fused_computation.180 | convolution fusion | flops 538968064 | bytes 3679232 | tf_op jit(solution)/shard_map/dot_general | solution.py:96
  47.5 2.2 reshape.336
  49.7 2.0 add_convert_fusion
  56.0 1.3 convert_reduce_fusion.2
  59.3 1.2 dynamic_slice.55
  61.3 1.6 constant_dynamic-update-slice_fusion.2
  63.0 1.3 fusion.139
  64.3 1.3 fusion.138
  66.6 1.4 fusion.97
  68.0 94.9 %all-gather.2.cloned.1.call-done = bf16[16384,512]{1,0:T(8,128)(2,1)} async-done(((bf16[1024,512]{1,0:T(8,128)(2,1)}), bf16[16384,512]{1,0:T(8,128)(2,1)}) %all-gather.2.cloned.1.call-update) | async-done | bytes 16777232 | tf_op jit(solution)/shard_map/all_gather | solution.py:94
  162.8 10.7 %gather_fusion = bf16[16,512,512]{2,1,0:T(8,128)(2,1)} fusion(bf16[32,512,512]{2,1,0:T(8,128)(2,1)} %bitcast.87, s32[1024]{0:T(1024)} %pad_clamp_fusion), kind=kCustom, calls=%fused_computation | custom fusion | bytes 16777280 | tf_op jit(solution)/shard_map/jit(_take)/gather | solution.py:133
  173.5 3.9 %fusion.135 = (bf16[8,512,512]{2,1,0:T(8,128)(2,1)S(1)}, bf16[8,512,512]{2,1,0:T(8,128)(2,1)S(1)}) fusion(bf16[16,512,512]{2,1,0:T(8,128)(2,1)} %gather_fusion), kind=kLoop, calls=%fused_computation.181 | loop fusion | bytes 16777216 | tf_op jit(solution)/shard_map/slice | solution.py:141
  177.4 2.4 fusion.142
  179.8 2.4 fusion.141
  182.2 4.6 %fusion.143 = (f32[512]{0:T(512)S(1)}, f32[512,4096]{1,0:T(8,128)}) fusion(bf16[4096,512]{1,0:T(8,128)(2,1)S(1)} %bitcast.92, bf16[512,2,128]{2,0,1:T(8,128)(2,1)S(1)} %copy-done.8, s32[512]{0:T(512)S(1)} %copy-done.9, s32[4096]{0:T(1024)S(1)} %get-tuple-element.28, pred[4096]{0:T(1024)(128)(4,1)S(1)} %copy-done.13), kind=kOutput, calls=%fused_computation.189 | convolution fusion | flops 547356160 | bytes 9592832 | tf_op jit(solution)/shard_map/qd,kd->qk/dot_general | solution.py:118
  186.8 3.6 %fusion.140 = (f32[512]{0:T(512)S(1)}, f32[512,4096]{1,0:T(8,128)S(1)}) fusion(bf16[4096,512]{1,0:T(8,128)(2,1)} %bitcast.93, bf16[512,2,128]{2,0,1:T(8,128)(2,1)S(1)} %copy-done.8, s32[512]{0:T(512)S(1)} %copy-done.9, s32[4096]{0:T(1024)S(1)} %get-tuple-element.28, pred[4096]{0:T(1024)(128)(4,1)S(1)} %copy-done.13), kind=kOutput, calls=%fused_computation.186 | convolution fusion | flops 547356160 | bytes 9592832 | tf_op jit(solution)/shard_map/qd,kd->qk/dot_general | solution.py:118
  190.4 11.0 %fusion.4 = (f32[512]{0:T(512)S(1)}, f32[512]{0:T(512)S(1)}, f32[512]{0:T(512)S(1)}, f32[512]{0:T(512)S(1)}) fusion(f32[512,4096]{1,0:T(8,128)S(1)} %get-tuple-element.64, f32[512]{0:T(512)S(1)} %get-tuple-element.63, s32[4096]{0:T(1024)S(1)} %get-tuple-element.27, s32[512]{0:T(512)S(1)} %copy-done.9, pred[4096]{0:T(1024)(128)(4,1)S(1)} %copy-done.12, ...), kind=kLoop, calls=%fused_computation.15 | loop fusion | flops 33552384 | bytes 33613824 | tf_op jit(solution)/shard_map/reduce_sum | solution.py:122
  201.4 5.6 %fusion.61 = f32[512,256]{1,0:T(8,128)S(1)} fusion(bf16[4096,512]{1,0:T(8,128)(2,1)} %bitcast.94, f32[512,4096]{1,0:T(8,128)} %get-tuple-element.68, f32[512]{0:T(512)S(1)} %get-tuple-element.67, s32[4096]{0:T(1024)S(1)} %get-tuple-element.28, s32[512]{0:T(512)S(1)} %copy-done.9, pred[4096]{0:T(1024)(128)(4,1)S(1)} %copy-done.13, f32[512]{0:T(512)S(1)} %bitcast.124), kind=kOutput, calls=%fused_computation.46 | convolution fusion | flops 1084358656 | bytes 11036672 | tf_op jit(solution)/shard_map/dot_general | solution.py:123
  207.1 3.9 %fusion.41 = f32[512,256]{1,0:T(8,128)S(1)} fusion(bf16[4096,512]{1,0:T(8,128)(2,1)} %bitcast.95, f32[512,4096]{1,0:T(8,128)S(1)} %get-tuple-element.62, f32[512]{0:T(512)S(1)} %get-tuple-element.61, s32[4096]{0:T(1024)S(1)} %get-tuple-element.28, s32[512]{0:T(512)S(1)} %copy-done.9, pred[4096]{0:T(1024)(128)(4,1)S(1)} %copy-done.13, f32[512]{0:T(512)S(1)} %bitcast.123), kind=kOutput, calls=%fused_computation.42 | convolution fusion | flops 1084358656 | bytes 11036672 | tf_op jit(solution)/shard_map/dot_general | solution.py:123
  211.1 2.4 fusion.85
  213.4 3.1 %multiply_reduce_fusion = (f32[512]{0:T(512)S(1)}, f32[512,256]{1,0:T(8,128)S(1)}) fusion(f32[512,256]{1,0:T(8,128)S(1)} %fusion.85, f32[512]{0:T(512)S(1)} %bitcast.117, f32[512,256]{1,0:T(8,128)S(1)} %fusion.61, f32[512]{0:T(512)S(1)} %bitcast.119, bf16[4096,512]{1,0:T(8,128)(2,1)S(1)} %bitcast.91, f32[512,4096]{1,0:T(8,128)S(1)} %get-tuple-element.64, ...), kind=kOutput, calls=%fused_computation.74 | convolution fusion | flops 1085406720 | bytes 12615684 | tf_op jit(solution)/shard_map/dot_general | solution.py:123
  218.5 1.7 convolution_convert_fusion
  221.0 66.2 %all-reduce.2.cloned.1.call-done = bf16[256,2048]{1,0:T(8,128)(2,1)} async-done(((bf16[256,2048]{1,0:T(8,128)(2,1)}), bf16[256,2048]{1,0:T(8,128)(2,1)}) %all-reduce.2.cloned.1.call-update) | async-done | bytes 1048592 | tf_op jit(solution)/shard_map/psum | solution.py:171
  287.2 2.6 fusion.19
  (96 shorter events, 24.1 us)
Async XLA Ops:
  7.2 211.3 %copy-start = (bf16[512,2048]{1,0:T(8,128)(2,1)S(1)}, bf16[512,2048]{1,0:T(8,128)(2,1)}, u32[]{:S(2)}) copy-start(bf16[512,2048]{1,0:T(8,128)(2,1)} %param.14) | copy-start | bytes 6291460
  7.2 155.7 %all-gather.2.cloned.1.call-start = ((), (), s32[]{:S(2)}) async-start(), calls=%async_computation | async-start | bytes 17825792 | tf_op jit(solution)/shard_map/all_gather | solution.py:94
  8.2 2.4 copy-start.14
  10.6 6.0 %copy-start.16 = (f32[2048]{0:T(1024)S(1)}, f32[2048]{0:T(1024)}, u32[]{:S(2)}) copy-start(f32[2048]{0:T(1024)} %param.10) | copy-start | bytes 24580
  14.2 5.9 %copy-start.5 = (f32[256,64]{1,0:T(8,128)}, f32[256,64]{1,0:T(8,128)S(1)}, u32[]{:S(2)}) copy-start(f32[256,64]{1,0:T(8,128)S(1)} %get-tuple-element.56) | copy-start | bytes 196612
  19.3 0.7 copy-start.6
  22.2 7.8 %collective-permute-start.1 = (bf16[256,2,256]{2,0,1:T(8,128)(2,1)}, bf16[256,2,256]{2,0,1:T(8,128)(2,1)S(1)}, u32[]{:S(2)}, u32[]{:S(2)}) collective-permute-start(bf16[256,2,256]{2,0,1:T(8,128)(2,1)} %get-tuple-element.47), channel_id=1, source_target_pairs={{0,32},{32,0},{1,33},{33,1},{2,34},{34,2},{3,35},{35,3},{4,36},{36... | collective-permute-start | bytes 786440 | tf_op jit(solution)/shard_map/ppermute | solution.py:85
  24.7 10.8 %collective-permute-start.2 = (bf16[256,2,256]{2,0,1:T(8,128)(2,1)S(1)}, bf16[256,2,256]{2,0,1:T(8,128)(2,1)}, u32[]{:S(2)}, u32[]{:S(2)}) collective-permute-start(bf16[256,2,256]{2,0,1:T(8,128)(2,1)S(1)} %get-tuple-element.48), channel_id=1, source_target_pairs={{0,32},{32,0},{1,33},{33,1},{2,34},{34,2},{3,35},{35,3},{4,36},{36... | collective-permute-start | bytes 786440 | tf_op jit(solution)/shard_map/ppermute | solution.py:85
  37.5 4.3 %collective-permute-start.3 = (bf16[512,512]{1,0:T(8,128)(2,1)}, bf16[512,512]{1,0:T(8,128)(2,1)}, u32[]{:S(2)}, u32[]{:S(2)}) collective-permute-start(bf16[512,512]{1,0:T(8,128)(2,1)} %get-tuple-element.39), channel_id=1, source_target_pairs={{0,4},{4,0},{1,5},{5,1},{2,6},{6,2},{3,7},{7,3},{8,12},{12,8},{9,1... | collective-permute-start | bytes 1572872 | tf_op jit(solution)/shard_map/ppermute | solution.py:39
  42.9 1.0 copy-start.1
  43.9 11.4 %copy-start.15 = (f32[4,2,128]{2,1,0:T(2,128)S(1)}, f32[4,2,128]{2,1,0:T(2,128)}, u32[]{:S(2)}) copy-start(f32[4,2,128]{2,1,0:T(2,128)} %param.15) | copy-start | bytes 12292
  43.9 19.1 %copy-start.2 = (bf16[2,512,512]{2,1,0:T(8,128)(2,1)S(1)}, bf16[2,512,512]{2,1,0:T(8,128)(2,1)}, u32[]{:S(2)}) copy-start(bf16[2,512,512]{2,1,0:T(8,128)(2,1)} %copy-done.1) | copy-start | bytes 3145732
  43.9 243.3 %all-reduce.2.cloned.1.call-start = ((), (), s32[]{:S(2)}) async-start(), calls=%async_computation.1 | async-start | bytes 2097152 | tf_op jit(solution)/shard_map/psum | solution.py:171
  53.1 8.3 %collective-permute-start = (bf16[256,2,128]{2,0,1:T(8,128)(2,1)}, bf16[256,2,128]{2,0,1:T(8,128)(2,1)}, u32[]{:S(2)}, u32[]{:S(2)}) collective-permute-start(bf16[256,2,128]{2,0,1:T(8,128)(2,1)} %bitcast.85), channel_id=1, source_target_pairs={{0,4},{4,0},{1,5},{5,1},{2,6},{6,2},{3,7},{7,3},{8,12},{12,8},{9,1... | collective-permute-start | bytes 393224 | tf_op jit(solution)/shard_map/ppermute | solution.py:39
  53.5 4.3 %copy-start.10 = (s32[512]{0:T(512)}, s32[512]{0:T(512)S(1)}, u32[]{:S(2)}) copy-start(s32[512]{0:T(512)S(1)} %iota_add_fusion.2) | copy-start | bytes 6148
  57.9 0.7 copy-start.7
  58.6 7.0 %copy-start.9 = (s32[512]{0:T(512)S(1)}, s32[512]{0:T(512)}, u32[]{:S(2)}) copy-start(s32[512]{0:T(512)} %convert_reduce_fusion.2) | copy-start | bytes 6148
  58.6 7.0 %copy-start.11 = (s32[512]{0:T(512)S(1)}, s32[512]{0:T(512)}, u32[]{:S(2)}) copy-start(s32[512]{0:T(512)} %copy-done.10) | copy-start | bytes 6148
  173.5 3.9 %copy-start.8 = (bf16[512,2,128]{2,0,1:T(8,128)(2,1)S(1)}, bf16[512,2,128]{2,0,1:T(8,128)(2,1)}, u32[]{:S(2)}) copy-start(bf16[512,2,128]{2,0,1:T(8,128)(2,1)} %constant_dynamic-update-slice_fusion.2) | copy-start | bytes 786436
  173.5 3.9 %copy-start.12 = (pred[4096]{0:T(1024)(128)(4,1)S(1)}, pred[4096]{0:T(1024)(128)(4,1)}, u32[]{:S(2)}) copy-start(pred[4096]{0:T(1024)(128)(4,1)} %broadcast_compare_fusion.1) | copy-start | bytes 12292
  177.4 4.8 %copy-start.4 = (bf16[8,512,512]{2,1,0:T(8,128)(2,1)}, bf16[8,512,512]{2,1,0:T(8,128)(2,1)S(1)}, u32[]{:S(2)}) copy-start(bf16[8,512,512]{2,1,0:T(8,128)(2,1)S(1)} %get-tuple-element.38) | copy-start | bytes 12582916
  179.8 2.4 copy-start.13
  207.1 4.0 %copy-start.17 = (f32[512,256]{1,0:T(8,128)S(1)}, f32[512,256]{1,0:T(8,128)}, u32[]{:S(2)}) copy-start(f32[512,256]{1,0:T(8,128)} %fusion.97) | copy-start | bytes 1572868
  216.5 70.7 %copy-start.3 = (bf16[256,2048]{1,0:T(8,128)(2,1)S(1)}, bf16[256,2048]{1,0:T(8,128)(2,1)}, u32[]{:S(2)}) copy-start(bf16[256,2048]{1,0:T(8,128)(2,1)} %param.9) | copy-start | bytes 3145732
  216.7 1.8 collective-permute-start.4
Sparse Core Ops, SparseCore 0:
  44.0 118.7 all-gather.1
  220.3 66.8 all-reduce.1

commit v8 on v7

--- a/solution.py
+++ b/solution.py
@@ -163,11 +163,9 @@
     ).astype(jnp.bfloat16)
     own_rows = lax.dynamic_slice_in_dim(head_out, core * rows, rows, axis=0)
     other_rows = swap_cores(lax.dynamic_slice_in_dim(head_out, (1 - core) * rows, rows, axis=0))
-    merged = jnp.where(
-        core == 0,
-        jnp.concatenate([own_rows, other_rows], axis=1),
-        jnp.concatenate([other_rows, own_rows], axis=1),
-    )
+    merged = jnp.zeros((rows, 2 * VD), head_out.dtype)
+    merged = lax.dynamic_update_slice_in_dim(merged, own_rows, core * VD, axis=1)
+    merged = lax.dynamic_update_slice_in_dim(merged, other_rows, (1 - core) * VD, axis=1)
     summed = lax.psum(
         jnp.dot(merged, w_out, preferred_element_type=jnp.float32).astype(jnp.bfloat16), "tp"
     ).astype(jnp.float32)

time: 297 us -> 297 us (level)
  no operation moved by 1% of the time
where the time goes in v8:
time: 297 us
  waiting for transfers between devices  173 us (58%)
  matrix products  43.2 us (15%)
  local copies, waits for them, and re-layouts  30.2 us (10%)
  other arithmetic  29.3 us (10%)
  between operations  14.5 us (5%)
  starting transfers between devices  6.13 us (2%)
    all_gather x1, waiting for transfers between devices, on_device(): gathered = lax.all_gather(kv_quad, ('y', 'x'), axis=0, tiled=True)  94.9 us
    psum x1, waiting for transfers between devices, on_device(): lax.psum(jnp.dot(merged, w_out, preferred_element_type=jnp.float32).astyp...  66.2 us
    dot_general x6, matrix products, stats_of(): jnp.dot(weights.astype(jnp.bfloat16), v_win, preferred_element_type=jnp.f...  17 us
    dot_general x6, matrix products, stats_of(): jnp.einsum('qd,kd->qk', q_pair[:, m, :], k_m, preferred_element_type=jnp....  15.6 us
    reduce_sum x2, other arithmetic, stats_of(): mass = jnp.sum(weights, axis=-1, keepdims=True)  11.4 us
    gather x1, local copies, waits for them, and re-layouts, on_device(): jnp.take(gathered.reshape(chips, span, -1), slot, axis=0, mode='clip')  10.7 us
    ppermute x2, waiting for transfers between devices, on_device(): lax.ppermute(kv_both[..., i * 2 * QK:(i + 1) * 2 * QK], 'z', [(0, 1), (1,...  10.6 us
  transfers between devices with their start and end apart: 7, of which 6 were waited for; matrix products, arithmetic and copies ran while one was open for 8% of the time, Pallas kernels for 0%

profile of v8, /device:TPU:1, one launch (start us, length us, event | category | flops | bytes accessed | tf_op | source)
XLA Modules:
  0.0 296.7 jit_solution(2216762492795552685)
XLA Ops:
  9.1 1.5 fusion.16
  10.6 2.7 fusion.124
  16.6 2.7 convolution_convert_fusion.1
  22.2 2.5 collective-permute-start.1
  24.8 5.1 %collective-permute-done.1 = bf16[256,2,256]{2,0,1:T(8,128)(2,1)S(1)} collective-permute-done((bf16[256,2,256]{2,0,1:T(8,128)(2,1)}, bf16[256,2,256]{2,0,1:T(8,128)(2,1)S(1)}, u32[]{:S(2)}, u32[]{:S(2)}) %collective-permute-start.1) | collective-permute-done | bytes 262176 | tf_op jit(solution)/shard_map/ppermute | solution.py:85
  30.0 5.5 %collective-permute-done.2 = bf16[256,2,256]{2,0,1:T(8,128)(2,1)} collective-permute-done((bf16[256,2,256]{2,0,1:T(8,128)(2,1)S(1)}, bf16[256,2,256]{2,0,1:T(8,128)(2,1)}, u32[]{:S(2)}, u32[]{:S(2)}) %collective-permute-start.2) | collective-permute-done | bytes 262176 | tf_op jit(solution)/shard_map/ppermute | solution.py:85
  37.5 2.4 collective-permute-start.3
  40.0 1.1 constant_dynamic-update-slice_fusion.1
  43.9 3.6 %fusion.126 = f32[256,512]{1,0:T(8,128)} fusion(bf16[2048,512]{1,0:T(8,128)(2,1)} %param.11, bf16[256,2048]{1,0:T(8,128)(2,1)} %param.9, f32[2048]{0:T(1024)S(1)} %copy-done.16, f32[256]{0:T(256)S(1)} %add_rsqrt_fusion.1), kind=kOutput, calls=%fused_computation.173 | convolution fusion | flops 538968064 | bytes 3679232 | tf_op jit(solution)/shard_map/dot_general | solution.py:96
  47.5 2.2 reshape.336
  49.7 2.0 add_convert_fusion
  56.0 1.3 convert_reduce_fusion.2
  59.3 1.2 dynamic_slice.55
  61.3 1.6 constant_dynamic-update-slice_fusion.2
  63.0 1.3 fusion.132
  64.3 1.3 fusion.131
  66.6 1.4 fusion.97
  68.0 94.9 %all-gather.2.cloned.1.call-done = bf16[16384,512]{1,0:T(8,128)(2,1)} async-done(((bf16[1024,512]{1,0:T(8,128)(2,1)}), bf16[16384,512]{1,0:T(8,128)(2,1)}) %all-gather.2.cloned.1.call-update) | async-done | bytes 16777232 | tf_op jit(solution)/shard_map/all_gather | solution.py:94
  162.8 10.7 %gather_fusion = bf16[16,512,512]{2,1,0:T(8,128)(2,1)} fusion(bf16[32,512,512]{2,1,0:T(8,128)(2,1)} %bitcast.88, s32[1024]{0:T(1024)} %pad_clamp_fusion), kind=kCustom, calls=%fused_computation | custom fusion | bytes 16777280 | tf_op jit(solution)/shard_map/jit(_take)/gather | solution.py:133
  173.5 3.9 %fusion.128 = (bf16[8,512,512]{2,1,0:T(8,128)(2,1)S(1)}, bf16[8,512,512]{2,1,0:T(8,128)(2,1)S(1)}) fusion(bf16[16,512,512]{2,1,0:T(8,128)(2,1)} %gather_fusion), kind=kLoop, calls=%fused_computation.174 | loop fusion | bytes 16777216 | tf_op jit(solution)/shard_map/slice | solution.py:141
  177.4 2.4 fusion.135
  179.8 2.4 fusion.134
  182.2 4.6 %fusion.136 = (f32[512]{0:T(512)S(1)}, f32[512,4096]{1,0:T(8,128)}) fusion(bf16[4096,512]{1,0:T(8,128)(2,1)S(1)} %bitcast.93, bf16[512,2,128]{2,0,1:T(8,128)(2,1)S(1)} %copy-done.8, s32[512]{0:T(512)S(1)} %copy-done.9, s32[4096]{0:T(1024)S(1)} %get-tuple-element.28, pred[4096]{0:T(1024)(128)(4,1)S(1)} %copy-done.13), kind=kOutput, calls=%fused_computation.182 | convolution fusion | flops 547356160 | bytes 9592832 | tf_op jit(solution)/shard_map/qd,kd->qk/dot_general | solution.py:118
  186.8 3.6 %fusion.133 = (f32[512]{0:T(512)S(1)}, f32[512,4096]{1,0:T(8,128)S(1)}) fusion(bf16[4096,512]{1,0:T(8,128)(2,1)} %bitcast.94, bf16[512,2,128]{2,0,1:T(8,128)(2,1)S(1)} %copy-done.8, s32[512]{0:T(512)S(1)} %copy-done.9, s32[4096]{0:T(1024)S(1)} %get-tuple-element.28, pred[4096]{0:T(1024)(128)(4,1)S(1)} %copy-done.13), kind=kOutput, calls=%fused_computation.179 | convolution fusion | flops 547356160 | bytes 9592832 | tf_op jit(solution)/shard_map/qd,kd->qk/dot_general | solution.py:118
  190.4 11.0 %fusion.4 = (f32[512]{0:T(512)S(1)}, f32[512]{0:T(512)S(1)}, f32[512]{0:T(512)S(1)}, f32[512]{0:T(512)S(1)}) fusion(f32[512,4096]{1,0:T(8,128)S(1)} %get-tuple-element.64, f32[512]{0:T(512)S(1)} %get-tuple-element.63, s32[4096]{0:T(1024)S(1)} %get-tuple-element.27, s32[512]{0:T(512)S(1)} %copy-done.9, pred[4096]{0:T(1024)(128)(4,1)S(1)} %copy-done.12, ...), kind=kLoop, calls=%fused_computation.15 | loop fusion | flops 33552384 | bytes 33613824 | tf_op jit(solution)/shard_map/reduce_sum | solution.py:122
  201.4 5.6 %fusion.61 = f32[512,256]{1,0:T(8,128)S(1)} fusion(bf16[4096,512]{1,0:T(8,128)(2,1)} %bitcast.95, f32[512,4096]{1,0:T(8,128)} %get-tuple-element.68, f32[512]{0:T(512)S(1)} %get-tuple-element.67, s32[4096]{0:T(1024)S(1)} %get-tuple-element.28, s32[512]{0:T(512)S(1)} %copy-done.9, pred[4096]{0:T(1024)(128)(4,1)S(1)} %copy-done.13, f32[512]{0:T(512)S(1)} %bitcast.125), kind=kOutput, calls=%fused_computation.46 | convolution fusion | flops 1084358656 | bytes 11036672 | tf_op jit(solution)/shard_map/dot_general | solution.py:123
  207.1 3.9 %fusion.41 = f32[512,256]{1,0:T(8,128)S(1)} fusion(bf16[4096,512]{1,0:T(8,128)(2,1)} %bitcast.96, f32[512,4096]{1,0:T(8,128)S(1)} %get-tuple-element.62, f32[512]{0:T(512)S(1)} %get-tuple-element.61, s32[4096]{0:T(1024)S(1)} %get-tuple-element.28, s32[512]{0:T(512)S(1)} %copy-done.9, pred[4096]{0:T(1024)(128)(4,1)S(1)} %copy-done.13, f32[512]{0:T(512)S(1)} %bitcast.124), kind=kOutput, calls=%fused_computation.42 | convolution fusion | flops 1084358656 | bytes 11036672 | tf_op jit(solution)/shard_map/dot_general | solution.py:123
  211.1 2.4 fusion.85
  213.4 3.1 %multiply_reduce_fusion = (f32[512]{0:T(512)S(1)}, f32[512,256]{1,0:T(8,128)S(1)}) fusion(f32[512,256]{1,0:T(8,128)S(1)} %fusion.85, f32[512]{0:T(512)S(1)} %bitcast.118, f32[512,256]{1,0:T(8,128)S(1)} %fusion.61, f32[512]{0:T(512)S(1)} %bitcast.120, bf16[4096,512]{1,0:T(8,128)(2,1)S(1)} %bitcast.92, f32[512,4096]{1,0:T(8,128)S(1)} %get-tuple-element.64, ...), kind=kOutput, calls=%fused_computation.74 | convolution fusion | flops 1085406720 | bytes 12615684 | tf_op jit(solution)/shard_map/dot_general | solution.py:123
  218.6 1.7 convolution_convert_fusion
  221.1 66.2 %all-reduce.2.cloned.1.call-done = bf16[256,2048]{1,0:T(8,128)(2,1)} async-done(((bf16[256,2048]{1,0:T(8,128)(2,1)}), bf16[256,2048]{1,0:T(8,128)(2,1)}) %all-reduce.2.cloned.1.call-update) | async-done | bytes 1048592 | tf_op jit(solution)/shard_map/psum | solution.py:169
  287.3 2.6 fusion.19
  (98 shorter events, 24.1 us)
Async XLA Ops:
  7.2 211.4 %copy-start = (bf16[512,2048]{1,0:T(8,128)(2,1)S(1)}, bf16[512,2048]{1,0:T(8,128)(2,1)}, u32[]{:S(2)}) copy-start(bf16[512,2048]{1,0:T(8,128)(2,1)} %param.14) | copy-start | bytes 6291460
  7.2 155.7 %all-gather.2.cloned.1.call-start = ((), (), s32[]{:S(2)}) async-start(), calls=%async_computation | async-start | bytes 17825792 | tf_op jit(solution)/shard_map/all_gather | solution.py:94
  8.2 2.4 copy-start.14
  10.6 6.0 %copy-start.16 = (f32[2048]{0:T(1024)S(1)}, f32[2048]{0:T(1024)}, u32[]{:S(2)}) copy-start(f32[2048]{0:T(1024)} %param.10) | copy-start | bytes 24580
  14.2 5.9 %copy-start.5 = (f32[256,64]{1,0:T(8,128)}, f32[256,64]{1,0:T(8,128)S(1)}, u32[]{:S(2)}) copy-start(f32[256,64]{1,0:T(8,128)S(1)} %get-tuple-element.56) | copy-start | bytes 196612
  19.3 0.7 copy-start.6
  22.2 7.8 %collective-permute-start.1 = (bf16[256,2,256]{2,0,1:T(8,128)(2,1)}, bf16[256,2,256]{2,0,1:T(8,128)(2,1)S(1)}, u32[]{:S(2)}, u32[]{:S(2)}) collective-permute-start(bf16[256,2,256]{2,0,1:T(8,128)(2,1)} %get-tuple-element.47), channel_id=1, source_target_pairs={{0,32},{32,0},{1,33},{33,1},{2,34},{34,2},{3,35},{35,3},{4,36},{36... | collective-permute-start | bytes 786440 | tf_op jit(solution)/shard_map/ppermute | solution.py:85
  24.7 10.8 %collective-permute-start.2 = (bf16[256,2,256]{2,0,1:T(8,128)(2,1)S(1)}, bf16[256,2,256]{2,0,1:T(8,128)(2,1)}, u32[]{:S(2)}, u32[]{:S(2)}) collective-permute-start(bf16[256,2,256]{2,0,1:T(8,128)(2,1)S(1)} %get-tuple-element.48), channel_id=1, source_target_pairs={{0,32},{32,0},{1,33},{33,1},{2,34},{34,2},{3,35},{35,3},{4,36},{36... | collective-permute-start | bytes 786440 | tf_op jit(solution)/shard_map/ppermute | solution.py:85
  37.5 4.3 %collective-permute-start.3 = (bf16[512,512]{1,0:T(8,128)(2,1)}, bf16[512,512]{1,0:T(8,128)(2,1)}, u32[]{:S(2)}, u32[]{:S(2)}) collective-permute-start(bf16[512,512]{1,0:T(8,128)(2,1)} %get-tuple-element.39), channel_id=1, source_target_pairs={{0,4},{4,0},{1,5},{5,1},{2,6},{6,2},{3,7},{7,3},{8,12},{12,8},{9,1... | collective-permute-start | bytes 1572872 | tf_op jit(solution)/shard_map/ppermute | solution.py:39
  42.9 1.0 copy-start.1
  43.9 11.4 %copy-start.15 = (f32[4,2,128]{2,1,0:T(2,128)S(1)}, f32[4,2,128]{2,1,0:T(2,128)}, u32[]{:S(2)}) copy-start(f32[4,2,128]{2,1,0:T(2,128)} %param.15) | copy-start | bytes 12292
  43.9 19.1 %copy-start.2 = (bf16[2,512,512]{2,1,0:T(8,128)(2,1)S(1)}, bf16[2,512,512]{2,1,0:T(8,128)(2,1)}, u32[]{:S(2)}) copy-start(bf16[2,512,512]{2,1,0:T(8,128)(2,1)} %copy-done.1) | copy-start | bytes 3145732
  43.9 243.4 %all-reduce.2.cloned.1.call-start = ((), (), s32[]{:S(2)}) async-start(), calls=%async_computation.1 | async-start | bytes 2097152 | tf_op jit(solution)/shard_map/psum | solution.py:169
  53.1 8.3 %collective-permute-start = (bf16[256,2,128]{2,0,1:T(8,128)(2,1)}, bf16[256,2,128]{2,0,1:T(8,128)(2,1)}, u32[]{:S(2)}, u32[]{:S(2)}) collective-permute-start(bf16[256,2,128]{2,0,1:T(8,128)(2,1)} %bitcast.86), channel_id=1, source_target_pairs={{0,4},{4,0},{1,5},{5,1},{2,6},{6,2},{3,7},{7,3},{8,12},{12,8},{9,1... | collective-permute-start | bytes 393224 | tf_op jit(solution)/shard_map/ppermute | solution.py:39
  53.5 4.3 %copy-start.10 = (s32[512]{0:T(512)}, s32[512]{0:T(512)S(1)}, u32[]{:S(2)}) copy-start(s32[512]{0:T(512)S(1)} %iota_add_fusion.2) | copy-start | bytes 6148
  57.9 0.7 copy-start.7
  58.6 7.0 %copy-start.9 = (s32[512]{0:T(512)S(1)}, s32[512]{0:T(512)}, u32[]{:S(2)}) copy-start(s32[512]{0:T(512)} %convert_reduce_fusion.2) | copy-start | bytes 6148
  58.6 7.0 %copy-start.11 = (s32[512]{0:T(512)S(1)}, s32[512]{0:T(512)}, u32[]{:S(2)}) copy-start(s32[512]{0:T(512)} %copy-done.10) | copy-start | bytes 6148
  173.5 3.9 %copy-start.8 = (bf16[512,2,128]{2,0,1:T(8,128)(2,1)S(1)}, bf16[512,2,128]{2,0,1:T(8,128)(2,1)}, u32[]{:S(2)}) copy-start(bf16[512,2,128]{2,0,1:T(8,128)(2,1)} %constant_dynamic-update-slice_fusion.2) | copy-start | bytes 786436
  173.5 3.9 %copy-start.12 = (pred[4096]{0:T(1024)(128)(4,1)S(1)}, pred[4096]{0:T(1024)(128)(4,1)}, u32[]{:S(2)}) copy-start(pred[4096]{0:T(1024)(128)(4,1)} %broadcast_compare_fusion.1) | copy-start | bytes 12292
  177.4 4.8 %copy-start.4 = (bf16[8,512,512]{2,1,0:T(8,128)(2,1)}, bf16[8,512,512]{2,1,0:T(8,128)(2,1)S(1)}, u32[]{:S(2)}) copy-start(bf16[8,512,512]{2,1,0:T(8,128)(2,1)S(1)} %get-tuple-element.38) | copy-start | bytes 12582916
  179.8 2.4 copy-start.13
  207.1 4.0 %copy-start.17 = (f32[512,256]{1,0:T(8,128)S(1)}, f32[512,256]{1,0:T(8,128)}, u32[]{:S(2)}) copy-start(f32[512,256]{1,0:T(8,128)} %fusion.97) | copy-start | bytes 1572868
  216.5 70.8 %copy-start.3 = (bf16[256,2048]{1,0:T(8,128)(2,1)S(1)}, bf16[256,2048]{1,0:T(8,128)(2,1)}, u32[]{:S(2)}) copy-start(bf16[256,2048]{1,0:T(8,128)(2,1)} %param.9) | copy-start | bytes 3145732
  216.8 1.8 collective-permute-start.4
Sparse Core Ops, SparseCore 0:
  44.0 118.7 all-gather.1
  220.4 66.8 all-reduce.1
